TPU v7x, 512 devices: a whole 4x8x8 slice. The times are simulated.
512 devices in a mesh: seg: 32 (over y, x), sec: 16 (over z, core).
Axes of the slice: x: 4, y: 8, z: 8, core: 2. Of those that a mesh axis runs over, the one named last changes fastest.
Arguments:
- blocks: bfloat16 [32, 4, 16, 128, 128], P('seg', None, 'sec'), may hold values from -0.5 to 0.5
- left_edge: bfloat16 [16, 128], P('sec'), may hold values from -0.5 to 0.5
- right_edge: bfloat16 [16, 128], P('sec'), may hold values from -6 to 6
- occupation: int32 [1024, 32], P(None, 'seg'), may hold values from 0 to 3
- start_sector: int32 [1024], replicated, may hold values from 0 to 15
Outputs:
- amplitude: float32 [1024], replicated
All inputs are finite; a program needn't handle non-finite values.
Results may differ from a plain program's by a relative error of at most 0.015.
Values may be sent and summed in bfloat16 or wider, within the bound.
No kernel may reach another device: no remote copies, remote signals or barrier semaphores. Data moves between devices by JAX's collectives and lax.ppermute only.
A program may use at most 64 MiB of HBM per device.

v0:
```python
import jax
import jax.numpy as jnp
from jax import lax
from jax.sharding import PartitionSpec as P


def padded_2(block, sides, width, periodic):
    for axis, dim in sides:
        count = lax.axis_size(axis)
        forward = [(i, i + 1) for i in range(count - 1)]
        if periodic:
            forward.append((count - 1, 0))
        backward = [(target, source) for source, target in forward]
        low = lax.ppermute(
            lax.slice_in_dim(block, block.shape[dim] - width, None, axis=dim), axis, forward
        )
        high = lax.ppermute(lax.slice_in_dim(block, 0, width, axis=dim), axis, backward)
        block = jnp.concatenate([low, block, high], axis=dim)
    return block


def state_masks(occ_site):
    levels = jnp.arange(4, dtype=jnp.int32)
    return (occ_site[:, None] == levels[None, :]).astype(jnp.float32)


def forward_send(vector, block_site, occ_masks):
    products = jnp.einsum("ka,nab->knb", vector, block_site, preferred_element_type=jnp.float32)
    terms = products * occ_masks[:, :, None]
    kept_term = (terms[:, 0] + terms[:, 3]).astype(jnp.bfloat16)
    upward = terms[:, 1].astype(jnp.bfloat16)
    downward = terms[:, 2].astype(jnp.bfloat16)
    return (kept_term, jnp.stack([downward, upward]))


def backward_send(vector, block_site, occ_masks):
    return (vector, jnp.stack([vector, vector]))


def forward_take(kept_term, padded, block_site, occ_masks):
    total = (
        kept_term.astype(jnp.float32)
        + padded[0].astype(jnp.float32)
        + padded[3].astype(jnp.float32)
    )
    return total.astype(jnp.bfloat16)


def backward_take(kept_term, padded, block_site, occ_masks):
    stacked = jnp.stack([kept_term, padded[3], padded[0], kept_term], axis=1)
    products = jnp.einsum("nab,knb->kna", block_site, stacked, preferred_element_type=jnp.float32)
    return jnp.sum(products * occ_masks[:, :, None], axis=1).astype(jnp.bfloat16)


def per_device(blocks, left_edge, right_edge, occupation, start_sector):
    seg_count = lax.axis_size("seg")
    half_count = seg_count // 2
    seg_index = lax.axis_index("seg")
    sec_index = lax.axis_index("sec")
    is_left = seg_index < half_count
    chain_depth = jnp.where(is_left, seg_index, seg_count - 1 - seg_index)
    is_first = chain_depth == 0
    meet_lower = seg_index == half_count - 1
    meet_upper = seg_index == half_count
    conf_count = occupation.shape[0]
    sites_here = occupation.shape[1]
    sector_width = blocks.shape[-1]
    block_count = 1
    columns = jnp.arange(sector_width, dtype=jnp.int32)
    lower_cols = (columns < sector_width // 2).astype(jnp.float32)
    upper_cols = 1.0 - lower_cols
    local_blocks = blocks[:, :, 0]
    left_row = left_edge[0]
    right_row = right_edge[0]
    batch_rows = conf_count // block_count

    def initial():
        zero_row = jnp.zeros_like(left_row)
        initial_left = jnp.where(
            (start_sector == sec_index)[:, None], left_row[None, :], zero_row[None, :]
        )
        initial_right = jnp.broadcast_to(right_row[None, :], (batch_rows, sector_width))
        return jnp.where(is_left, initial_left, initial_right)

    def run_sites(vector):
        position = jnp.where(is_left, 0, sites_here - 1)
        block_site = lax.dynamic_index_in_dim(local_blocks, position, 0, keepdims=False)
        occ_site = lax.dynamic_index_in_dim(occupation, position, 1, keepdims=False)
        occ_masks = state_masks(occ_site)
        kept_term, outgoing = lax.cond(
            is_left, forward_send, backward_send, vector, block_site, occ_masks
        )
        padded = padded_2(outgoing, (("sec", 0),), 1, True)
        vector = lax.cond(
            is_left, forward_take, backward_take, kept_term, padded, block_site, occ_masks
        )
        return vector

    section_count = half_count + block_count - 1

    def section(section_index, state_pair):
        incoming, partial_value = state_pair
        batch_index = section_index - chain_depth
        is_valid = (batch_index >= 0) & (batch_index < block_count)
        vector = jnp.where(is_first, initial(), incoming)
        vector = run_sites(vector)
        padded = padded_2(vector[None], (("seg", 0),), 1, False)
        received = jnp.where(is_left, padded[0], padded[2])
        own_vals = vector.astype(jnp.float32)
        lower_part = jnp.sum(own_vals * padded[2].astype(jnp.float32) * lower_cols[None, :], axis=1)
        upper_part = jnp.sum(own_vals * padded[0].astype(jnp.float32) * upper_cols[None, :], axis=1)
        product = jnp.where(meet_lower, lower_part, upper_part)
        previous = partial_value
        store_here = (meet_lower | meet_upper) & is_valid
        partial_value = jnp.where(store_here, product, previous)
        return (received, partial_value)

    start_state = (
        jnp.zeros((batch_rows, sector_width), jnp.bfloat16),
        jnp.zeros((conf_count,), jnp.float32),
    )
    final_state = lax.fori_loop(0, section_count, section, start_state)
    return lax.psum(final_state[1], ("seg", "sec"))


def solution(mesh):
    in_specs = (
        P("seg", None, "sec", None, None),
        P("sec", None),
        P("sec", None),
        P(None, "seg"),
        P(),
    )
    out_specs = P()
    return jax.shard_map(
        per_device, mesh=mesh, in_specs=in_specs, out_specs=out_specs, check_vma=False
    )
```

profile of v0, /device:TPU:1, one launch (start us, length us, event | category | flops | bytes accessed | tf_op | source)
XLA Modules:
  0.0 528.2 jit_solution(16015874300515925806)
XLA Ops:
  0.0 413.8 %while.18 = (s32[]{:T(128)}, bf16[1024,128]{1,0:T(8,128)(2,1)S(1)}, f32[1024]{0:T(1024)S(1)}, pred[]{:T(512)}, pred[]{:T(512)}, /*index=5*/s32[]{:T(128)}, s32[1...) while((s32[]{:T(128)}, bf16[1024,128]{1,0:T(8,128)(2,1)S(1)}, ...), condition=%wide.region_8.9_spmd.clone, body=%wide.region_0.8_spmd.clone.sunk | while | flops 274213504 | bytes 16602105 | solution.py:122
  4.2 6.8 %collective-permute-start = (bf16[1,1024,128]{2,1,0:T(8,128)(2,1)S(1)}, bf16[1,1024,128]{2,1,0:T(8,128)(2,1)S(1)}, u32[]{:S(2)}, u32[]{:S(2)}) collective-permute-start(bf16[1,1024,128]{2,1,0:T(8,128)(2,1)S(1)} %get-tuple-element.627), channel_id=1, source_target_pairs={{1,0},{2,1},{3,2},{4,3},{5,4},{6,5},{7,6},{8,7},{9,8},{10,9},{11,1... | collective-permute-start | bytes 786440 | tf_op jit(solution)/shard_map/while/body/eval_jaxpr/ppermute | solution.py:17
  21.7 3.8 collective-permute-done.3
  30.1 7.4 %collective-permute-start = (bf16[1,1024,128]{2,1,0:T(8,128)(2,1)S(1)}, bf16[1,1024,128]{2,1,0:T(8,128)(2,1)S(1)}, u32[]{:S(2)}, u32[]{:S(2)}) collective-permute-start(bf16[1,1024,128]{2,1,0:T(8,128)(2,1)S(1)} %get-tuple-element.627), channel_id=1, source_target_pairs={{1,0},{2,1},{3,2},{4,3},{5,4},{6,5},{7,6},{8,7},{9,8},{10,9},{11,1... | collective-permute-start | bytes 786440 | tf_op jit(solution)/shard_map/while/body/eval_jaxpr/ppermute | solution.py:17
  47.4 3.8 collective-permute-done.3
  55.8 6.6 %collective-permute-start = (bf16[1,1024,128]{2,1,0:T(8,128)(2,1)S(1)}, bf16[1,1024,128]{2,1,0:T(8,128)(2,1)S(1)}, u32[]{:S(2)}, u32[]{:S(2)}) collective-permute-start(bf16[1,1024,128]{2,1,0:T(8,128)(2,1)S(1)} %get-tuple-element.627), channel_id=1, source_target_pairs={{1,0},{2,1},{3,2},{4,3},{5,4},{6,5},{7,6},{8,7},{9,8},{10,9},{11,1... | collective-permute-start | bytes 786440 | tf_op jit(solution)/shard_map/while/body/eval_jaxpr/ppermute | solution.py:17
  65.8 4.4 collective-permute-start.2
  73.5 4.1 collective-permute-done.3
  82.1 6.6 %collective-permute-start = (bf16[1,1024,128]{2,1,0:T(8,128)(2,1)S(1)}, bf16[1,1024,128]{2,1,0:T(8,128)(2,1)S(1)}, u32[]{:S(2)}, u32[]{:S(2)}) collective-permute-start(bf16[1,1024,128]{2,1,0:T(8,128)(2,1)S(1)} %get-tuple-element.627), channel_id=1, source_target_pairs={{1,0},{2,1},{3,2},{4,3},{5,4},{6,5},{7,6},{8,7},{9,8},{10,9},{11,1... | collective-permute-start | bytes 786440 | tf_op jit(solution)/shard_map/while/body/eval_jaxpr/ppermute | solution.py:17
  92.2 3.8 collective-permute-start.2
  99.2 4.1 collective-permute-done.3
  107.9 6.4 %collective-permute-start = (bf16[1,1024,128]{2,1,0:T(8,128)(2,1)S(1)}, bf16[1,1024,128]{2,1,0:T(8,128)(2,1)S(1)}, u32[]{:S(2)}, u32[]{:S(2)}) collective-permute-start(bf16[1,1024,128]{2,1,0:T(8,128)(2,1)S(1)} %get-tuple-element.627), channel_id=1, source_target_pairs={{1,0},{2,1},{3,2},{4,3},{5,4},{6,5},{7,6},{8,7},{9,8},{10,9},{11,1... | collective-permute-start | bytes 786440 | tf_op jit(solution)/shard_map/while/body/eval_jaxpr/ppermute | solution.py:17
  117.8 3.7 collective-permute-start.2
  124.7 4.0 collective-permute-done.3
  133.2 6.4 %collective-permute-start = (bf16[1,1024,128]{2,1,0:T(8,128)(2,1)S(1)}, bf16[1,1024,128]{2,1,0:T(8,128)(2,1)S(1)}, u32[]{:S(2)}, u32[]{:S(2)}) collective-permute-start(bf16[1,1024,128]{2,1,0:T(8,128)(2,1)S(1)} %get-tuple-element.627), channel_id=1, source_target_pairs={{1,0},{2,1},{3,2},{4,3},{5,4},{6,5},{7,6},{8,7},{9,8},{10,9},{11,1... | collective-permute-start | bytes 786440 | tf_op jit(solution)/shard_map/while/body/eval_jaxpr/ppermute | solution.py:17
  143.1 3.6 collective-permute-start.2
  149.9 4.0 collective-permute-done.3
  158.5 6.3 %collective-permute-start = (bf16[1,1024,128]{2,1,0:T(8,128)(2,1)S(1)}, bf16[1,1024,128]{2,1,0:T(8,128)(2,1)S(1)}, u32[]{:S(2)}, u32[]{:S(2)}) collective-permute-start(bf16[1,1024,128]{2,1,0:T(8,128)(2,1)S(1)} %get-tuple-element.627), channel_id=1, source_target_pairs={{1,0},{2,1},{3,2},{4,3},{5,4},{6,5},{7,6},{8,7},{9,8},{10,9},{11,1... | collective-permute-start | bytes 786440 | tf_op jit(solution)/shard_map/while/body/eval_jaxpr/ppermute | solution.py:17
  168.3 3.6 collective-permute-start.2
  175.1 4.1 collective-permute-done.3
  183.7 6.3 %collective-permute-start = (bf16[1,1024,128]{2,1,0:T(8,128)(2,1)S(1)}, bf16[1,1024,128]{2,1,0:T(8,128)(2,1)S(1)}, u32[]{:S(2)}, u32[]{:S(2)}) collective-permute-start(bf16[1,1024,128]{2,1,0:T(8,128)(2,1)S(1)} %get-tuple-element.627), channel_id=1, source_target_pairs={{1,0},{2,1},{3,2},{4,3},{5,4},{6,5},{7,6},{8,7},{9,8},{10,9},{11,1... | collective-permute-start | bytes 786440 | tf_op jit(solution)/shard_map/while/body/eval_jaxpr/ppermute | solution.py:17
  193.4 3.6 collective-permute-start.2
  200.3 4.1 collective-permute-done.3
  208.9 6.2 %collective-permute-start = (bf16[1,1024,128]{2,1,0:T(8,128)(2,1)S(1)}, bf16[1,1024,128]{2,1,0:T(8,128)(2,1)S(1)}, u32[]{:S(2)}, u32[]{:S(2)}) collective-permute-start(bf16[1,1024,128]{2,1,0:T(8,128)(2,1)S(1)} %get-tuple-element.627), channel_id=1, source_target_pairs={{1,0},{2,1},{3,2},{4,3},{5,4},{6,5},{7,6},{8,7},{9,8},{10,9},{11,1... | collective-permute-start | bytes 786440 | tf_op jit(solution)/shard_map/while/body/eval_jaxpr/ppermute | solution.py:17
  218.6 3.6 collective-permute-start.2
  225.5 4.1 collective-permute-done.3
  234.1 6.2 %collective-permute-start = (bf16[1,1024,128]{2,1,0:T(8,128)(2,1)S(1)}, bf16[1,1024,128]{2,1,0:T(8,128)(2,1)S(1)}, u32[]{:S(2)}, u32[]{:S(2)}) collective-permute-start(bf16[1,1024,128]{2,1,0:T(8,128)(2,1)S(1)} %get-tuple-element.627), channel_id=1, source_target_pairs={{1,0},{2,1},{3,2},{4,3},{5,4},{6,5},{7,6},{8,7},{9,8},{10,9},{11,1... | collective-permute-start | bytes 786440 | tf_op jit(solution)/shard_map/while/body/eval_jaxpr/ppermute | solution.py:17
  243.7 3.6 collective-permute-start.2
  250.6 4.1 collective-permute-done.3
  259.2 6.2 %collective-permute-start = (bf16[1,1024,128]{2,1,0:T(8,128)(2,1)S(1)}, bf16[1,1024,128]{2,1,0:T(8,128)(2,1)S(1)}, u32[]{:S(2)}, u32[]{:S(2)}) collective-permute-start(bf16[1,1024,128]{2,1,0:T(8,128)(2,1)S(1)} %get-tuple-element.627), channel_id=1, source_target_pairs={{1,0},{2,1},{3,2},{4,3},{5,4},{6,5},{7,6},{8,7},{9,8},{10,9},{11,1... | collective-permute-start | bytes 786440 | tf_op jit(solution)/shard_map/while/body/eval_jaxpr/ppermute | solution.py:17
  268.8 3.8 collective-permute-start.2
  275.9 4.4 collective-permute-done.3
  284.8 6.2 %collective-permute-start = (bf16[1,1024,128]{2,1,0:T(8,128)(2,1)S(1)}, bf16[1,1024,128]{2,1,0:T(8,128)(2,1)S(1)}, u32[]{:S(2)}, u32[]{:S(2)}) collective-permute-start(bf16[1,1024,128]{2,1,0:T(8,128)(2,1)S(1)} %get-tuple-element.627), channel_id=1, source_target_pairs={{1,0},{2,1},{3,2},{4,3},{5,4},{6,5},{7,6},{8,7},{9,8},{10,9},{11,1... | collective-permute-start | bytes 786440 | tf_op jit(solution)/shard_map/while/body/eval_jaxpr/ppermute | solution.py:17
  294.4 6.0 %collective-permute-start.2 = (bf16[1,1024,128]{2,1,0:T(8,128)(2,1)S(1)}, bf16[1,1024,128]{2,1,0:T(8,128)(2,1)S(1)}, u32[]{:S(2)}, u32[]{:S(2)}) collective-permute-start(bf16[1,1024,128]{2,1,0:T(8,128)(2,1)S(1)} %bitcast.59), channel_id=1, source_target_pairs={{0,16},{16,32},{32,48},{48,64},{64,80},{80,96},{96,112},{112,128},... | collective-permute-start | bytes 786440 | tf_op jit(solution)/shard_map/while/body/eval_jaxpr/ppermute | solution.py:14
  303.7 4.1 collective-permute-done.3
  312.3 6.4 %collective-permute-start = (bf16[1,1024,128]{2,1,0:T(8,128)(2,1)S(1)}, bf16[1,1024,128]{2,1,0:T(8,128)(2,1)S(1)}, u32[]{:S(2)}, u32[]{:S(2)}) collective-permute-start(bf16[1,1024,128]{2,1,0:T(8,128)(2,1)S(1)} %get-tuple-element.627), channel_id=1, source_target_pairs={{1,0},{2,1},{3,2},{4,3},{5,4},{6,5},{7,6},{8,7},{9,8},{10,9},{11,1... | collective-permute-start | bytes 786440 | tf_op jit(solution)/shard_map/while/body/eval_jaxpr/ppermute | solution.py:17
  322.2 4.7 collective-permute-start.2
  330.1 4.1 collective-permute-done.3
  338.8 6.4 %collective-permute-start = (bf16[1,1024,128]{2,1,0:T(8,128)(2,1)S(1)}, bf16[1,1024,128]{2,1,0:T(8,128)(2,1)S(1)}, u32[]{:S(2)}, u32[]{:S(2)}) collective-permute-start(bf16[1,1024,128]{2,1,0:T(8,128)(2,1)S(1)} %get-tuple-element.627), channel_id=1, source_target_pairs={{1,0},{2,1},{3,2},{4,3},{5,4},{6,5},{7,6},{8,7},{9,8},{10,9},{11,1... | collective-permute-start | bytes 786440 | tf_op jit(solution)/shard_map/while/body/eval_jaxpr/ppermute | solution.py:17
  348.6 4.6 collective-permute-start.2
  356.5 4.1 collective-permute-done.3
  365.2 6.4 %collective-permute-start = (bf16[1,1024,128]{2,1,0:T(8,128)(2,1)S(1)}, bf16[1,1024,128]{2,1,0:T(8,128)(2,1)S(1)}, u32[]{:S(2)}, u32[]{:S(2)}) collective-permute-start(bf16[1,1024,128]{2,1,0:T(8,128)(2,1)S(1)} %get-tuple-element.627), channel_id=1, source_target_pairs={{1,0},{2,1},{3,2},{4,3},{5,4},{6,5},{7,6},{8,7},{9,8},{10,9},{11,1... | collective-permute-start | bytes 786440 | tf_op jit(solution)/shard_map/while/body/eval_jaxpr/ppermute | solution.py:17
  375.0 4.7 collective-permute-start.2
  383.0 4.1 collective-permute-done.3
  391.6 6.4 %collective-permute-start = (bf16[1,1024,128]{2,1,0:T(8,128)(2,1)S(1)}, bf16[1,1024,128]{2,1,0:T(8,128)(2,1)S(1)}, u32[]{:S(2)}, u32[]{:S(2)}) collective-permute-start(bf16[1,1024,128]{2,1,0:T(8,128)(2,1)S(1)} %get-tuple-element.627), channel_id=1, source_target_pairs={{1,0},{2,1},{3,2},{4,3},{5,4},{6,5},{7,6},{8,7},{9,8},{10,9},{11,1... | collective-permute-start | bytes 786440 | tf_op jit(solution)/shard_map/while/body/eval_jaxpr/ppermute | solution.py:17
  401.5 4.6 collective-permute-start.2
  409.3 4.1 collective-permute-done.3
  413.8 114.3 %psum.7 = f32[1024]{0:T(1024)} all-reduce(f32[1024]{0:T(1024)S(1)} %get-tuple-element.425), channel_id=1, replica_groups=mesh['seg'=32,'sec'=16] {'seg','sec'}, use_global_device_ids=true, to_apply=%region_9.10 | all-reduce | flops 1024 | bytes 8192 | tf_op jit(solution)/shard_map/psum | solution.py:123
  (340 shorter events, 215.7 us)
Async XLA Ops:
  4.2 8.0 %collective-permute-start = (bf16[1,1024,128]{2,1,0:T(8,128)(2,1)S(1)}, bf16[1,1024,128]{2,1,0:T(8,128)(2,1)S(1)}, u32[]{:S(2)}, u32[]{:S(2)}) collective-permute-start(bf16[1,1024,128]{2,1,0:T(8,128)(2,1)S(1)} %get-tuple-element.627), channel_id=1, source_target_pairs={{1,0},{2,1},{3,2},{4,3},{5,4},{6,5},{7,6},{8,7},{9,8},{10,9},{11,1... | collective-permute-start | bytes 786440 | tf_op jit(solution)/shard_map/while/body/eval_jaxpr/ppermute | solution.py:17
  15.3 6.4 %collective-permute-start.2 = (bf16[1,1024,128]{2,1,0:T(8,128)(2,1)S(1)}, bf16[1,1024,128]{2,1,0:T(8,128)(2,1)S(1)}, u32[]{:S(2)}, u32[]{:S(2)}) collective-permute-start(bf16[1,1024,128]{2,1,0:T(8,128)(2,1)S(1)} %bitcast.59), channel_id=1, source_target_pairs={{0,16},{16,32},{32,48},{48,64},{64,80},{80,96},{96,112},{112,128},... | collective-permute-start | bytes 786440 | tf_op jit(solution)/shard_map/while/body/eval_jaxpr/ppermute | solution.py:14
  18.5 7.1 %collective-permute-start.3 = (bf16[1,1024,128]{2,1,0:T(8,128)(2,1)S(1)}, bf16[1,1024,128]{2,1,0:T(8,128)(2,1)S(1)}, u32[]{:S(2)}, u32[]{:S(2)}) collective-permute-start(bf16[1,1024,128]{2,1,0:T(8,128)(2,1)S(1)} %bitcast.60), channel_id=1, source_target_pairs={{16,0},{32,16},{48,32},{64,48},{80,64},{96,80},{112,96},{128,112},... | collective-permute-start | bytes 786440 | tf_op jit(solution)/shard_map/while/body/eval_jaxpr/ppermute | solution.py:17
  30.1 8.6 %collective-permute-start = (bf16[1,1024,128]{2,1,0:T(8,128)(2,1)S(1)}, bf16[1,1024,128]{2,1,0:T(8,128)(2,1)S(1)}, u32[]{:S(2)}, u32[]{:S(2)}) collective-permute-start(bf16[1,1024,128]{2,1,0:T(8,128)(2,1)S(1)} %get-tuple-element.627), channel_id=1, source_target_pairs={{1,0},{2,1},{3,2},{4,3},{5,4},{6,5},{7,6},{8,7},{9,8},{10,9},{11,1... | collective-permute-start | bytes 786440 | tf_op jit(solution)/shard_map/while/body/eval_jaxpr/ppermute | solution.py:17
  41.0 6.4 %collective-permute-start.2 = (bf16[1,1024,128]{2,1,0:T(8,128)(2,1)S(1)}, bf16[1,1024,128]{2,1,0:T(8,128)(2,1)S(1)}, u32[]{:S(2)}, u32[]{:S(2)}) collective-permute-start(bf16[1,1024,128]{2,1,0:T(8,128)(2,1)S(1)} %bitcast.59), channel_id=1, source_target_pairs={{0,16},{16,32},{32,48},{48,64},{64,80},{80,96},{96,112},{112,128},... | collective-permute-start | bytes 786440 | tf_op jit(solution)/shard_map/while/body/eval_jaxpr/ppermute | solution.py:14
  44.1 7.1 %collective-permute-start.3 = (bf16[1,1024,128]{2,1,0:T(8,128)(2,1)S(1)}, bf16[1,1024,128]{2,1,0:T(8,128)(2,1)S(1)}, u32[]{:S(2)}, u32[]{:S(2)}) collective-permute-start(bf16[1,1024,128]{2,1,0:T(8,128)(2,1)S(1)} %bitcast.60), channel_id=1, source_target_pairs={{16,0},{32,16},{48,32},{64,48},{80,64},{96,80},{112,96},{128,112},... | collective-permute-start | bytes 786440 | tf_op jit(solution)/shard_map/while/body/eval_jaxpr/ppermute | solution.py:17
  55.8 8.0 %collective-permute-start = (bf16[1,1024,128]{2,1,0:T(8,128)(2,1)S(1)}, bf16[1,1024,128]{2,1,0:T(8,128)(2,1)S(1)}, u32[]{:S(2)}, u32[]{:S(2)}) collective-permute-start(bf16[1,1024,128]{2,1,0:T(8,128)(2,1)S(1)} %get-tuple-element.627), channel_id=1, source_target_pairs={{1,0},{2,1},{3,2},{4,3},{5,4},{6,5},{7,6},{8,7},{9,8},{10,9},{11,1... | collective-permute-start | bytes 786440 | tf_op jit(solution)/shard_map/while/body/eval_jaxpr/ppermute | solution.py:17
  65.8 7.7 %collective-permute-start.2 = (bf16[1,1024,128]{2,1,0:T(8,128)(2,1)S(1)}, bf16[1,1024,128]{2,1,0:T(8,128)(2,1)S(1)}, u32[]{:S(2)}, u32[]{:S(2)}) collective-permute-start(bf16[1,1024,128]{2,1,0:T(8,128)(2,1)S(1)} %bitcast.59), channel_id=1, source_target_pairs={{0,16},{16,32},{32,48},{48,64},{64,80},{80,96},{96,112},{112,128},... | collective-permute-start | bytes 786440 | tf_op jit(solution)/shard_map/while/body/eval_jaxpr/ppermute | solution.py:14
  70.2 7.4 %collective-permute-start.3 = (bf16[1,1024,128]{2,1,0:T(8,128)(2,1)S(1)}, bf16[1,1024,128]{2,1,0:T(8,128)(2,1)S(1)}, u32[]{:S(2)}, u32[]{:S(2)}) collective-permute-start(bf16[1,1024,128]{2,1,0:T(8,128)(2,1)S(1)} %bitcast.60), channel_id=1, source_target_pairs={{16,0},{32,16},{48,32},{64,48},{80,64},{96,80},{112,96},{128,112},... | collective-permute-start | bytes 786440 | tf_op jit(solution)/shard_map/while/body/eval_jaxpr/ppermute | solution.py:17
  82.1 7.8 %collective-permute-start = (bf16[1,1024,128]{2,1,0:T(8,128)(2,1)S(1)}, bf16[1,1024,128]{2,1,0:T(8,128)(2,1)S(1)}, u32[]{:S(2)}, u32[]{:S(2)}) collective-permute-start(bf16[1,1024,128]{2,1,0:T(8,128)(2,1)S(1)} %get-tuple-element.627), channel_id=1, source_target_pairs={{1,0},{2,1},{3,2},{4,3},{5,4},{6,5},{7,6},{8,7},{9,8},{10,9},{11,1... | collective-permute-start | bytes 786440 | tf_op jit(solution)/shard_map/while/body/eval_jaxpr/ppermute | solution.py:17
  92.2 7.0 %collective-permute-start.2 = (bf16[1,1024,128]{2,1,0:T(8,128)(2,1)S(1)}, bf16[1,1024,128]{2,1,0:T(8,128)(2,1)S(1)}, u32[]{:S(2)}, u32[]{:S(2)}) collective-permute-start(bf16[1,1024,128]{2,1,0:T(8,128)(2,1)S(1)} %bitcast.59), channel_id=1, source_target_pairs={{0,16},{16,32},{32,48},{48,64},{64,80},{80,96},{96,112},{112,128},... | collective-permute-start | bytes 786440 | tf_op jit(solution)/shard_map/while/body/eval_jaxpr/ppermute | solution.py:14
  96.0 7.4 %collective-permute-start.3 = (bf16[1,1024,128]{2,1,0:T(8,128)(2,1)S(1)}, bf16[1,1024,128]{2,1,0:T(8,128)(2,1)S(1)}, u32[]{:S(2)}, u32[]{:S(2)}) collective-permute-start(bf16[1,1024,128]{2,1,0:T(8,128)(2,1)S(1)} %bitcast.60), channel_id=1, source_target_pairs={{16,0},{32,16},{48,32},{64,48},{80,64},{96,80},{112,96},{128,112},... | collective-permute-start | bytes 786440 | tf_op jit(solution)/shard_map/while/body/eval_jaxpr/ppermute | solution.py:17
  107.9 7.7 %collective-permute-start = (bf16[1,1024,128]{2,1,0:T(8,128)(2,1)S(1)}, bf16[1,1024,128]{2,1,0:T(8,128)(2,1)S(1)}, u32[]{:S(2)}, u32[]{:S(2)}) collective-permute-start(bf16[1,1024,128]{2,1,0:T(8,128)(2,1)S(1)} %get-tuple-element.627), channel_id=1, source_target_pairs={{1,0},{2,1},{3,2},{4,3},{5,4},{6,5},{7,6},{8,7},{9,8},{10,9},{11,1... | collective-permute-start | bytes 786440 | tf_op jit(solution)/shard_map/while/body/eval_jaxpr/ppermute | solution.py:17
  117.8 7.0 %collective-permute-start.2 = (bf16[1,1024,128]{2,1,0:T(8,128)(2,1)S(1)}, bf16[1,1024,128]{2,1,0:T(8,128)(2,1)S(1)}, u32[]{:S(2)}, u32[]{:S(2)}) collective-permute-start(bf16[1,1024,128]{2,1,0:T(8,128)(2,1)S(1)} %bitcast.59), channel_id=1, source_target_pairs={{0,16},{16,32},{32,48},{48,64},{64,80},{80,96},{96,112},{112,128},... | collective-permute-start | bytes 786440 | tf_op jit(solution)/shard_map/while/body/eval_jaxpr/ppermute | solution.py:14
  121.4 7.2 %collective-permute-start.3 = (bf16[1,1024,128]{2,1,0:T(8,128)(2,1)S(1)}, bf16[1,1024,128]{2,1,0:T(8,128)(2,1)S(1)}, u32[]{:S(2)}, u32[]{:S(2)}) collective-permute-start(bf16[1,1024,128]{2,1,0:T(8,128)(2,1)S(1)} %bitcast.60), channel_id=1, source_target_pairs={{16,0},{32,16},{48,32},{64,48},{80,64},{96,80},{112,96},{128,112},... | collective-permute-start | bytes 786440 | tf_op jit(solution)/shard_map/while/body/eval_jaxpr/ppermute | solution.py:17
  133.2 7.9 %collective-permute-start = (bf16[1,1024,128]{2,1,0:T(8,128)(2,1)S(1)}, bf16[1,1024,128]{2,1,0:T(8,128)(2,1)S(1)}, u32[]{:S(2)}, u32[]{:S(2)}) collective-permute-start(bf16[1,1024,128]{2,1,0:T(8,128)(2,1)S(1)} %get-tuple-element.627), channel_id=1, source_target_pairs={{1,0},{2,1},{3,2},{4,3},{5,4},{6,5},{7,6},{8,7},{9,8},{10,9},{11,1... | collective-permute-start | bytes 786440 | tf_op jit(solution)/shard_map/while/body/eval_jaxpr/ppermute | solution.py:17
  143.1 6.8 %collective-permute-start.2 = (bf16[1,1024,128]{2,1,0:T(8,128)(2,1)S(1)}, bf16[1,1024,128]{2,1,0:T(8,128)(2,1)S(1)}, u32[]{:S(2)}, u32[]{:S(2)}) collective-permute-start(bf16[1,1024,128]{2,1,0:T(8,128)(2,1)S(1)} %bitcast.59), channel_id=1, source_target_pairs={{0,16},{16,32},{32,48},{48,64},{64,80},{80,96},{96,112},{112,128},... | collective-permute-start | bytes 786440 | tf_op jit(solution)/shard_map/while/body/eval_jaxpr/ppermute | solution.py:14
  146.6 7.3 %collective-permute-start.3 = (bf16[1,1024,128]{2,1,0:T(8,128)(2,1)S(1)}, bf16[1,1024,128]{2,1,0:T(8,128)(2,1)S(1)}, u32[]{:S(2)}, u32[]{:S(2)}) collective-permute-start(bf16[1,1024,128]{2,1,0:T(8,128)(2,1)S(1)} %bitcast.60), channel_id=1, source_target_pairs={{16,0},{32,16},{48,32},{64,48},{80,64},{96,80},{112,96},{128,112},... | collective-permute-start | bytes 786440 | tf_op jit(solution)/shard_map/while/body/eval_jaxpr/ppermute | solution.py:17
  158.5 7.8 %collective-permute-start = (bf16[1,1024,128]{2,1,0:T(8,128)(2,1)S(1)}, bf16[1,1024,128]{2,1,0:T(8,128)(2,1)S(1)}, u32[]{:S(2)}, u32[]{:S(2)}) collective-permute-start(bf16[1,1024,128]{2,1,0:T(8,128)(2,1)S(1)} %get-tuple-element.627), channel_id=1, source_target_pairs={{1,0},{2,1},{3,2},{4,3},{5,4},{6,5},{7,6},{8,7},{9,8},{10,9},{11,1... | collective-permute-start | bytes 786440 | tf_op jit(solution)/shard_map/while/body/eval_jaxpr/ppermute | solution.py:17
  168.3 6.9 %collective-permute-start.2 = (bf16[1,1024,128]{2,1,0:T(8,128)(2,1)S(1)}, bf16[1,1024,128]{2,1,0:T(8,128)(2,1)S(1)}, u32[]{:S(2)}, u32[]{:S(2)}) collective-permute-start(bf16[1,1024,128]{2,1,0:T(8,128)(2,1)S(1)} %bitcast.59), channel_id=1, source_target_pairs={{0,16},{16,32},{32,48},{48,64},{64,80},{80,96},{96,112},{112,128},... | collective-permute-start | bytes 786440 | tf_op jit(solution)/shard_map/while/body/eval_jaxpr/ppermute | solution.py:14
  171.8 7.3 %collective-permute-start.3 = (bf16[1,1024,128]{2,1,0:T(8,128)(2,1)S(1)}, bf16[1,1024,128]{2,1,0:T(8,128)(2,1)S(1)}, u32[]{:S(2)}, u32[]{:S(2)}) collective-permute-start(bf16[1,1024,128]{2,1,0:T(8,128)(2,1)S(1)} %bitcast.60), channel_id=1, source_target_pairs={{16,0},{32,16},{48,32},{64,48},{80,64},{96,80},{112,96},{128,112},... | collective-permute-start | bytes 786440 | tf_op jit(solution)/shard_map/while/body/eval_jaxpr/ppermute | solution.py:17
  183.7 7.8 %collective-permute-start = (bf16[1,1024,128]{2,1,0:T(8,128)(2,1)S(1)}, bf16[1,1024,128]{2,1,0:T(8,128)(2,1)S(1)}, u32[]{:S(2)}, u32[]{:S(2)}) collective-permute-start(bf16[1,1024,128]{2,1,0:T(8,128)(2,1)S(1)} %get-tuple-element.627), channel_id=1, source_target_pairs={{1,0},{2,1},{3,2},{4,3},{5,4},{6,5},{7,6},{8,7},{9,8},{10,9},{11,1... | collective-permute-start | bytes 786440 | tf_op jit(solution)/shard_map/while/body/eval_jaxpr/ppermute | solution.py:17
  193.4 6.9 %collective-permute-start.2 = (bf16[1,1024,128]{2,1,0:T(8,128)(2,1)S(1)}, bf16[1,1024,128]{2,1,0:T(8,128)(2,1)S(1)}, u32[]{:S(2)}, u32[]{:S(2)}) collective-permute-start(bf16[1,1024,128]{2,1,0:T(8,128)(2,1)S(1)} %bitcast.59), channel_id=1, source_target_pairs={{0,16},{16,32},{32,48},{48,64},{64,80},{80,96},{96,112},{112,128},... | collective-permute-start | bytes 786440 | tf_op jit(solution)/shard_map/while/body/eval_jaxpr/ppermute | solution.py:14
  197.0 7.4 %collective-permute-start.3 = (bf16[1,1024,128]{2,1,0:T(8,128)(2,1)S(1)}, bf16[1,1024,128]{2,1,0:T(8,128)(2,1)S(1)}, u32[]{:S(2)}, u32[]{:S(2)}) collective-permute-start(bf16[1,1024,128]{2,1,0:T(8,128)(2,1)S(1)} %bitcast.60), channel_id=1, source_target_pairs={{16,0},{32,16},{48,32},{64,48},{80,64},{96,80},{112,96},{128,112},... | collective-permute-start | bytes 786440 | tf_op jit(solution)/shard_map/while/body/eval_jaxpr/ppermute | solution.py:17
  208.9 7.7 %collective-permute-start = (bf16[1,1024,128]{2,1,0:T(8,128)(2,1)S(1)}, bf16[1,1024,128]{2,1,0:T(8,128)(2,1)S(1)}, u32[]{:S(2)}, u32[]{:S(2)}) collective-permute-start(bf16[1,1024,128]{2,1,0:T(8,128)(2,1)S(1)} %get-tuple-element.627), channel_id=1, source_target_pairs={{1,0},{2,1},{3,2},{4,3},{5,4},{6,5},{7,6},{8,7},{9,8},{10,9},{11,1... | collective-permute-start | bytes 786440 | tf_op jit(solution)/shard_map/while/body/eval_jaxpr/ppermute | solution.py:17
  218.6 6.9 %collective-permute-start.2 = (bf16[1,1024,128]{2,1,0:T(8,128)(2,1)S(1)}, bf16[1,1024,128]{2,1,0:T(8,128)(2,1)S(1)}, u32[]{:S(2)}, u32[]{:S(2)}) collective-permute-start(bf16[1,1024,128]{2,1,0:T(8,128)(2,1)S(1)} %bitcast.59), channel_id=1, source_target_pairs={{0,16},{16,32},{32,48},{48,64},{64,80},{80,96},{96,112},{112,128},... | collective-permute-start | bytes 786440 | tf_op jit(solution)/shard_map/while/body/eval_jaxpr/ppermute | solution.py:14
  222.2 7.4 %collective-permute-start.3 = (bf16[1,1024,128]{2,1,0:T(8,128)(2,1)S(1)}, bf16[1,1024,128]{2,1,0:T(8,128)(2,1)S(1)}, u32[]{:S(2)}, u32[]{:S(2)}) collective-permute-start(bf16[1,1024,128]{2,1,0:T(8,128)(2,1)S(1)} %bitcast.60), channel_id=1, source_target_pairs={{16,0},{32,16},{48,32},{64,48},{80,64},{96,80},{112,96},{128,112},... | collective-permute-start | bytes 786440 | tf_op jit(solution)/shard_map/while/body/eval_jaxpr/ppermute | solution.py:17
  234.1 7.7 %collective-permute-start = (bf16[1,1024,128]{2,1,0:T(8,128)(2,1)S(1)}, bf16[1,1024,128]{2,1,0:T(8,128)(2,1)S(1)}, u32[]{:S(2)}, u32[]{:S(2)}) collective-permute-start(bf16[1,1024,128]{2,1,0:T(8,128)(2,1)S(1)} %get-tuple-element.627), channel_id=1, source_target_pairs={{1,0},{2,1},{3,2},{4,3},{5,4},{6,5},{7,6},{8,7},{9,8},{10,9},{11,1... | collective-permute-start | bytes 786440 | tf_op jit(solution)/shard_map/while/body/eval_jaxpr/ppermute | solution.py:17
  243.7 6.9 %collective-permute-start.2 = (bf16[1,1024,128]{2,1,0:T(8,128)(2,1)S(1)}, bf16[1,1024,128]{2,1,0:T(8,128)(2,1)S(1)}, u32[]{:S(2)}, u32[]{:S(2)}) collective-permute-start(bf16[1,1024,128]{2,1,0:T(8,128)(2,1)S(1)} %bitcast.59), channel_id=1, source_target_pairs={{0,16},{16,32},{32,48},{48,64},{64,80},{80,96},{96,112},{112,128},... | collective-permute-start | bytes 786440 | tf_op jit(solution)/shard_map/while/body/eval_jaxpr/ppermute | solution.py:14
  247.3 7.4 %collective-permute-start.3 = (bf16[1,1024,128]{2,1,0:T(8,128)(2,1)S(1)}, bf16[1,1024,128]{2,1,0:T(8,128)(2,1)S(1)}, u32[]{:S(2)}, u32[]{:S(2)}) collective-permute-start(bf16[1,1024,128]{2,1,0:T(8,128)(2,1)S(1)} %bitcast.60), channel_id=1, source_target_pairs={{16,0},{32,16},{48,32},{64,48},{80,64},{96,80},{112,96},{128,112},... | collective-permute-start | bytes 786440 | tf_op jit(solution)/shard_map/while/body/eval_jaxpr/ppermute | solution.py:17
  259.2 7.7 %collective-permute-start = (bf16[1,1024,128]{2,1,0:T(8,128)(2,1)S(1)}, bf16[1,1024,128]{2,1,0:T(8,128)(2,1)S(1)}, u32[]{:S(2)}, u32[]{:S(2)}) collective-permute-start(bf16[1,1024,128]{2,1,0:T(8,128)(2,1)S(1)} %get-tuple-element.627), channel_id=1, source_target_pairs={{1,0},{2,1},{3,2},{4,3},{5,4},{6,5},{7,6},{8,7},{9,8},{10,9},{11,1... | collective-permute-start | bytes 786440 | tf_op jit(solution)/shard_map/while/body/eval_jaxpr/ppermute | solution.py:17
  268.8 7.1 %collective-permute-start.2 = (bf16[1,1024,128]{2,1,0:T(8,128)(2,1)S(1)}, bf16[1,1024,128]{2,1,0:T(8,128)(2,1)S(1)}, u32[]{:S(2)}, u32[]{:S(2)}) collective-permute-start(bf16[1,1024,128]{2,1,0:T(8,128)(2,1)S(1)} %bitcast.59), channel_id=1, source_target_pairs={{0,16},{16,32},{32,48},{48,64},{64,80},{80,96},{96,112},{112,128},... | collective-permute-start | bytes 786440 | tf_op jit(solution)/shard_map/while/body/eval_jaxpr/ppermute | solution.py:14
  272.6 7.7 %collective-permute-start.3 = (bf16[1,1024,128]{2,1,0:T(8,128)(2,1)S(1)}, bf16[1,1024,128]{2,1,0:T(8,128)(2,1)S(1)}, u32[]{:S(2)}, u32[]{:S(2)}) collective-permute-start(bf16[1,1024,128]{2,1,0:T(8,128)(2,1)S(1)} %bitcast.60), channel_id=1, source_target_pairs={{16,0},{32,16},{48,32},{64,48},{80,64},{96,80},{112,96},{128,112},... | collective-permute-start | bytes 786440 | tf_op jit(solution)/shard_map/while/body/eval_jaxpr/ppermute | solution.py:17
  284.8 7.7 %collective-permute-start = (bf16[1,1024,128]{2,1,0:T(8,128)(2,1)S(1)}, bf16[1,1024,128]{2,1,0:T(8,128)(2,1)S(1)}, u32[]{:S(2)}, u32[]{:S(2)}) collective-permute-start(bf16[1,1024,128]{2,1,0:T(8,128)(2,1)S(1)} %get-tuple-element.627), channel_id=1, source_target_pairs={{1,0},{2,1},{3,2},{4,3},{5,4},{6,5},{7,6},{8,7},{9,8},{10,9},{11,1... | collective-permute-start | bytes 786440 | tf_op jit(solution)/shard_map/while/body/eval_jaxpr/ppermute | solution.py:17
  294.4 9.3 %collective-permute-start.2 = (bf16[1,1024,128]{2,1,0:T(8,128)(2,1)S(1)}, bf16[1,1024,128]{2,1,0:T(8,128)(2,1)S(1)}, u32[]{:S(2)}, u32[]{:S(2)}) collective-permute-start(bf16[1,1024,128]{2,1,0:T(8,128)(2,1)S(1)} %bitcast.59), channel_id=1, source_target_pairs={{0,16},{16,32},{32,48},{48,64},{64,80},{80,96},{96,112},{112,128},... | collective-permute-start | bytes 786440 | tf_op jit(solution)/shard_map/while/body/eval_jaxpr/ppermute | solution.py:14
  300.4 7.4 %collective-permute-start.3 = (bf16[1,1024,128]{2,1,0:T(8,128)(2,1)S(1)}, bf16[1,1024,128]{2,1,0:T(8,128)(2,1)S(1)}, u32[]{:S(2)}, u32[]{:S(2)}) collective-permute-start(bf16[1,1024,128]{2,1,0:T(8,128)(2,1)S(1)} %bitcast.60), channel_id=1, source_target_pairs={{16,0},{32,16},{48,32},{64,48},{80,64},{96,80},{112,96},{128,112},... | collective-permute-start | bytes 786440 | tf_op jit(solution)/shard_map/while/body/eval_jaxpr/ppermute | solution.py:17
  312.3 7.7 %collective-permute-start = (bf16[1,1024,128]{2,1,0:T(8,128)(2,1)S(1)}, bf16[1,1024,128]{2,1,0:T(8,128)(2,1)S(1)}, u32[]{:S(2)}, u32[]{:S(2)}) collective-permute-start(bf16[1,1024,128]{2,1,0:T(8,128)(2,1)S(1)} %get-tuple-element.627), channel_id=1, source_target_pairs={{1,0},{2,1},{3,2},{4,3},{5,4},{6,5},{7,6},{8,7},{9,8},{10,9},{11,1... | collective-permute-start | bytes 786440 | tf_op jit(solution)/shard_map/while/body/eval_jaxpr/ppermute | solution.py:17
  322.2 8.0 %collective-permute-start.2 = (bf16[1,1024,128]{2,1,0:T(8,128)(2,1)S(1)}, bf16[1,1024,128]{2,1,0:T(8,128)(2,1)S(1)}, u32[]{:S(2)}, u32[]{:S(2)}) collective-permute-start(bf16[1,1024,128]{2,1,0:T(8,128)(2,1)S(1)} %bitcast.59), channel_id=1, source_target_pairs={{0,16},{16,32},{32,48},{48,64},{64,80},{80,96},{96,112},{112,128},... | collective-permute-start | bytes 786440 | tf_op jit(solution)/shard_map/while/body/eval_jaxpr/ppermute | solution.py:14
  326.8 7.4 %collective-permute-start.3 = (bf16[1,1024,128]{2,1,0:T(8,128)(2,1)S(1)}, bf16[1,1024,128]{2,1,0:T(8,128)(2,1)S(1)}, u32[]{:S(2)}, u32[]{:S(2)}) collective-permute-start(bf16[1,1024,128]{2,1,0:T(8,128)(2,1)S(1)} %bitcast.60), channel_id=1, source_target_pairs={{16,0},{32,16},{48,32},{64,48},{80,64},{96,80},{112,96},{128,112},... | collective-permute-start | bytes 786440 | tf_op jit(solution)/shard_map/while/body/eval_jaxpr/ppermute | solution.py:17
  338.8 7.7 %collective-permute-start = (bf16[1,1024,128]{2,1,0:T(8,128)(2,1)S(1)}, bf16[1,1024,128]{2,1,0:T(8,128)(2,1)S(1)}, u32[]{:S(2)}, u32[]{:S(2)}) collective-permute-start(bf16[1,1024,128]{2,1,0:T(8,128)(2,1)S(1)} %get-tuple-element.627), channel_id=1, source_target_pairs={{1,0},{2,1},{3,2},{4,3},{5,4},{6,5},{7,6},{8,7},{9,8},{10,9},{11,1... | collective-permute-start | bytes 786440 | tf_op jit(solution)/shard_map/while/body/eval_jaxpr/ppermute | solution.py:17
  348.6 7.9 %collective-permute-start.2 = (bf16[1,1024,128]{2,1,0:T(8,128)(2,1)S(1)}, bf16[1,1024,128]{2,1,0:T(8,128)(2,1)S(1)}, u32[]{:S(2)}, u32[]{:S(2)}) collective-permute-start(bf16[1,1024,128]{2,1,0:T(8,128)(2,1)S(1)} %bitcast.59), channel_id=1, source_target_pairs={{0,16},{16,32},{32,48},{48,64},{64,80},{80,96},{96,112},{112,128},... | collective-permute-start | bytes 786440 | tf_op jit(solution)/shard_map/while/body/eval_jaxpr/ppermute | solution.py:14
  353.2 7.4 %collective-permute-start.3 = (bf16[1,1024,128]{2,1,0:T(8,128)(2,1)S(1)}, bf16[1,1024,128]{2,1,0:T(8,128)(2,1)S(1)}, u32[]{:S(2)}, u32[]{:S(2)}) collective-permute-start(bf16[1,1024,128]{2,1,0:T(8,128)(2,1)S(1)} %bitcast.60), channel_id=1, source_target_pairs={{16,0},{32,16},{48,32},{64,48},{80,64},{96,80},{112,96},{128,112},... | collective-permute-start | bytes 786440 | tf_op jit(solution)/shard_map/while/body/eval_jaxpr/ppermute | solution.py:17
  365.2 7.7 %collective-permute-start = (bf16[1,1024,128]{2,1,0:T(8,128)(2,1)S(1)}, bf16[1,1024,128]{2,1,0:T(8,128)(2,1)S(1)}, u32[]{:S(2)}, u32[]{:S(2)}) collective-permute-start(bf16[1,1024,128]{2,1,0:T(8,128)(2,1)S(1)} %get-tuple-element.627), channel_id=1, source_target_pairs={{1,0},{2,1},{3,2},{4,3},{5,4},{6,5},{7,6},{8,7},{9,8},{10,9},{11,1... | collective-permute-start | bytes 786440 | tf_op jit(solution)/shard_map/while/body/eval_jaxpr/ppermute | solution.py:17
  375.0 7.9 %collective-permute-start.2 = (bf16[1,1024,128]{2,1,0:T(8,128)(2,1)S(1)}, bf16[1,1024,128]{2,1,0:T(8,128)(2,1)S(1)}, u32[]{:S(2)}, u32[]{:S(2)}) collective-permute-start(bf16[1,1024,128]{2,1,0:T(8,128)(2,1)S(1)} %bitcast.59), channel_id=1, source_target_pairs={{0,16},{16,32},{32,48},{48,64},{64,80},{80,96},{96,112},{112,128},... | collective-permute-start | bytes 786440 | tf_op jit(solution)/shard_map/while/body/eval_jaxpr/ppermute | solution.py:14
  379.7 7.4 %collective-permute-start.3 = (bf16[1,1024,128]{2,1,0:T(8,128)(2,1)S(1)}, bf16[1,1024,128]{2,1,0:T(8,128)(2,1)S(1)}, u32[]{:S(2)}, u32[]{:S(2)}) collective-permute-start(bf16[1,1024,128]{2,1,0:T(8,128)(2,1)S(1)} %bitcast.60), channel_id=1, source_target_pairs={{16,0},{32,16},{48,32},{64,48},{80,64},{96,80},{112,96},{128,112},... | collective-permute-start | bytes 786440 | tf_op jit(solution)/shard_map/while/body/eval_jaxpr/ppermute | solution.py:17
  391.6 7.7 %collective-permute-start = (bf16[1,1024,128]{2,1,0:T(8,128)(2,1)S(1)}, bf16[1,1024,128]{2,1,0:T(8,128)(2,1)S(1)}, u32[]{:S(2)}, u32[]{:S(2)}) collective-permute-start(bf16[1,1024,128]{2,1,0:T(8,128)(2,1)S(1)} %get-tuple-element.627), channel_id=1, source_target_pairs={{1,0},{2,1},{3,2},{4,3},{5,4},{6,5},{7,6},{8,7},{9,8},{10,9},{11,1... | collective-permute-start | bytes 786440 | tf_op jit(solution)/shard_map/while/body/eval_jaxpr/ppermute | solution.py:17
  401.5 7.9 %collective-permute-start.2 = (bf16[1,1024,128]{2,1,0:T(8,128)(2,1)S(1)}, bf16[1,1024,128]{2,1,0:T(8,128)(2,1)S(1)}, u32[]{:S(2)}, u32[]{:S(2)}) collective-permute-start(bf16[1,1024,128]{2,1,0:T(8,128)(2,1)S(1)} %bitcast.59), channel_id=1, source_target_pairs={{0,16},{16,32},{32,48},{48,64},{64,80},{80,96},{96,112},{112,128},... | collective-permute-start | bytes 786440 | tf_op jit(solution)/shard_map/while/body/eval_jaxpr/ppermute | solution.py:14
  406.0 7.4 %collective-permute-start.3 = (bf16[1,1024,128]{2,1,0:T(8,128)(2,1)S(1)}, bf16[1,1024,128]{2,1,0:T(8,128)(2,1)S(1)}, u32[]{:S(2)}, u32[]{:S(2)}) collective-permute-start(bf16[1,1024,128]{2,1,0:T(8,128)(2,1)S(1)} %bitcast.60), channel_id=1, source_target_pairs={{16,0},{32,16},{48,32},{64,48},{80,64},{96,80},{112,96},{128,112},... | collective-permute-start | bytes 786440 | tf_op jit(solution)/shard_map/while/body/eval_jaxpr/ppermute | solution.py:17
  (16 other events, 54.0 us)
where the time goes:
time: 531 us; the launch traced here: 528 us
  starting transfers between devices  188 us (35%)
  waiting for transfers between devices  150 us (28%)
  blocking collectives  114 us (21%)
  other arithmetic  45.8 us (9%)
  matrix products  26 us (5%)
    ppermute x32, starting transfers between devices, padded_2(): lax.ppermute(lax.slice_in_dim(block, 0, width, axis=dim), axis, backward)  124 us
    psum x1, blocking collectives, per_device(): return lax.psum(final_state[1], ('seg', 'sec'))  114 us
    ppermute x32, waiting for transfers between devices, padded_2(): lax.ppermute(lax.slice_in_dim(block, 0, width, axis=dim), axis, backward)  86.9 us
    ppermute x32, starting transfers between devices, padded_2(): lax.ppermute(lax.slice_in_dim(block, block.shape[dim] - width, None, axis...  64.2 us
    ppermute x32, waiting for transfers between devices, padded_2(): lax.ppermute(lax.slice_in_dim(block, block.shape[dim] - width, None, axis...  63 us
    dot_general x16, matrix products, forward_send(): jnp.einsum('ka,nab->knb', vector, block_site, preferred_element_type=jnp....  26 us
    select_n x16, other arithmetic, section(): vector = jnp.where(is_first, initial(), incoming)  14 us
    convert_element_type x16, other arithmetic, state_masks(): return (occ_site[:, None] == levels[None, :]).astype(jnp.float32)  11.1 us
  transfers between devices with their start and end apart: 64, of which 64 were waited for; matrix products, arithmetic and copies ran while one was open for 0% of the time, Pallas kernels for 0%

commit v1 on v0

--- a/solution.py
+++ b/solution.py
@@ -120,7 +120,7 @@
         jnp.zeros((conf_count,), jnp.float32),
     )
     final_state = lax.fori_loop(0, section_count, section, start_state)
-    return lax.psum(final_state[1], ("seg", "sec"))
+    return jnp.sum(lax.all_gather(final_state[1], ("seg", "sec")), axis=0)
 
 
 def solution(mesh):

time: 531 us -> 561 us (1.056)
  blocking collectives: 114 us -> 0 us
  waiting for transfers between devices: 150 us -> 251 us
  starting transfers between devices: 188 us -> 214 us
  between operations: 0.01 us -> 13.4 us
    all_gather x0 -> x1, waiting for transfers between devices: none -> 146 us  [per_device(): return jnp.sum(lax.all_gather(final_state[1], ('seg', 'sec')), axis=0)]
    psum x1 -> x0, blocking collectives: 114 us -> none  [per_device(): return lax.psum(final_state[1], ('seg', 'sec'))]
    ppermute x32, starting transfers between devices: 64.2 us -> 103 us  [padded_2(): lax.ppermute(lax.slice_in_dim(block, block.shape[dim] - width, None, axis...]
    ppermute x32, waiting for transfers between devices: 86.9 us -> 57.4 us  [padded_2(): lax.ppermute(lax.slice_in_dim(block, 0, width, axis=dim), axis, backward)]
    ppermute x32, waiting for transfers between devices: 63 us -> 48.3 us  [padded_2(): lax.ppermute(lax.slice_in_dim(block, block.shape[dim] - width, None, axis...]
    ppermute x32, starting transfers between devices: 124 us -> 111 us  [padded_2(): lax.ppermute(lax.slice_in_dim(block, 0, width, axis=dim), axis, backward)]
  transfers between devices with their start and end apart: 64 -> 65, of which waited for: 64 -> 65; matrix products, arithmetic and copies ran while one was open for 0% -> 0% of each run, Pallas kernels for 0% -> 0%
where the time goes in v1:
time: 561 us; the launch traced here: 558 us
  waiting for transfers between devices  251 us (45%)
  starting transfers between devices  214 us (38%)
  other arithmetic  46.5 us (8%)
  matrix products  26 us (5%)
  between operations  13.4 us (2%)
    all_gather x1, waiting for transfers between devices, per_device(): return jnp.sum(lax.all_gather(final_state[1], ('seg', 'sec')), axis=0)  146 us
    ppermute x32, starting transfers between devices, padded_2(): lax.ppermute(lax.slice_in_dim(block, 0, width, axis=dim), axis, backward)  111 us
    ppermute x32, starting transfers between devices, padded_2(): lax.ppermute(lax.slice_in_dim(block, block.shape[dim] - width, None, axis...  103 us
    ppermute x32, waiting for transfers between devices, padded_2(): lax.ppermute(lax.slice_in_dim(block, 0, width, axis=dim), axis, backward)  57.4 us
    ppermute x32, waiting for transfers between devices, padded_2(): lax.ppermute(lax.slice_in_dim(block, block.shape[dim] - width, None, axis...  48.3 us
    dot_general x16, matrix products, forward_send(): jnp.einsum('ka,nab->knb', vector, block_site, preferred_element_type=jnp....  26 us
    select_n x16, other arithmetic, section(): vector = jnp.where(is_first, initial(), incoming)  14 us
  transfers between devices with their start and end apart: 65, of which 65 were waited for; matrix products, arithmetic and copies ran while one was open for 0% of the time, Pallas kernels for 0%

profile of v1, /device:TPU:1, one launch (start us, length us, event | category | flops | bytes accessed | tf_op | source)
XLA Modules:
  0.0 557.9 jit_solution(2948368375429976423)
XLA Ops:
  6.6 395.8 %while.18 = (s32[]{:T(128)}, bf16[1024,128]{1,0:T(8,128)(2,1)S(1)}, f32[1024]{0:T(1024)S(1)}, pred[]{:T(512)}, pred[]{:T(512)}, /*index=5*/s32[]{:T(128)}, s32[1...) while((s32[]{:T(128)}, bf16[1024,128]{1,0:T(8,128)(2,1)S(1)}, ...), condition=%wide.region_8.9_spmd.clone, body=%wide.region_0.8_spmd.clone.sunk | while | flops 274213504 | bytes 16602105 | solution.py:122
  10.7 6.9 %collective-permute-start = (bf16[1,1024,128]{2,1,0:T(8,128)(2,1)S(1)}, bf16[1,1024,128]{2,1,0:T(8,128)(2,1)S(1)}, u32[]{:S(2)}, u32[]{:S(2)}) collective-permute-start(bf16[1,1024,128]{2,1,0:T(8,128)(2,1)S(1)} %get-tuple-element.627), channel_id=1, source_target_pairs={{1,0},{2,1},{3,2},{4,3},{5,4},{6,5},{7,6},{8,7},{9,8},{10,9},{11,1... | collective-permute-start | bytes 786440 | tf_op jit(solution)/shard_map/while/body/eval_jaxpr/ppermute | solution.py:17
  18.7 3.0 collective-permute-done.1
  23.1 4.0 collective-permute-start.2
  35.0 7.1 %collective-permute-start = (bf16[1,1024,128]{2,1,0:T(8,128)(2,1)S(1)}, bf16[1,1024,128]{2,1,0:T(8,128)(2,1)S(1)}, u32[]{:S(2)}, u32[]{:S(2)}) collective-permute-start(bf16[1,1024,128]{2,1,0:T(8,128)(2,1)S(1)} %get-tuple-element.627), channel_id=1, source_target_pairs={{1,0},{2,1},{3,2},{4,3},{5,4},{6,5},{7,6},{8,7},{9,8},{10,9},{11,1... | collective-permute-start | bytes 786440 | tf_op jit(solution)/shard_map/while/body/eval_jaxpr/ppermute | solution.py:17
  43.3 2.2 collective-permute-done.1
  46.9 4.8 collective-permute-start.2
  59.4 6.0 %collective-permute-start = (bf16[1,1024,128]{2,1,0:T(8,128)(2,1)S(1)}, bf16[1,1024,128]{2,1,0:T(8,128)(2,1)S(1)}, u32[]{:S(2)}, u32[]{:S(2)}) collective-permute-start(bf16[1,1024,128]{2,1,0:T(8,128)(2,1)S(1)} %get-tuple-element.627), channel_id=1, source_target_pairs={{1,0},{2,1},{3,2},{4,3},{5,4},{6,5},{7,6},{8,7},{9,8},{10,9},{11,1... | collective-permute-start | bytes 786440 | tf_op jit(solution)/shard_map/while/body/eval_jaxpr/ppermute | solution.py:17
  66.9 1.9 collective-permute-done.1
  70.2 4.8 collective-permute-start.2
  82.8 6.3 %collective-permute-start = (bf16[1,1024,128]{2,1,0:T(8,128)(2,1)S(1)}, bf16[1,1024,128]{2,1,0:T(8,128)(2,1)S(1)}, u32[]{:S(2)}, u32[]{:S(2)}) collective-permute-start(bf16[1,1024,128]{2,1,0:T(8,128)(2,1)S(1)} %get-tuple-element.627), channel_id=1, source_target_pairs={{1,0},{2,1},{3,2},{4,3},{5,4},{6,5},{7,6},{8,7},{9,8},{10,9},{11,1... | collective-permute-start | bytes 786440 | tf_op jit(solution)/shard_map/while/body/eval_jaxpr/ppermute | solution.py:17
  90.3 2.2 collective-permute-done.1
  93.8 4.8 collective-permute-start.2
  106.4 5.9 %collective-permute-start = (bf16[1,1024,128]{2,1,0:T(8,128)(2,1)S(1)}, bf16[1,1024,128]{2,1,0:T(8,128)(2,1)S(1)}, u32[]{:S(2)}, u32[]{:S(2)}) collective-permute-start(bf16[1,1024,128]{2,1,0:T(8,128)(2,1)S(1)} %get-tuple-element.627), channel_id=1, source_target_pairs={{1,0},{2,1},{3,2},{4,3},{5,4},{6,5},{7,6},{8,7},{9,8},{10,9},{11,1... | collective-permute-start | bytes 786440 | tf_op jit(solution)/shard_map/while/body/eval_jaxpr/ppermute | solution.py:17
  117.0 6.0 %collective-permute-start.2 = (bf16[1,1024,128]{2,1,0:T(8,128)(2,1)S(1)}, bf16[1,1024,128]{2,1,0:T(8,128)(2,1)S(1)}, u32[]{:S(2)}, u32[]{:S(2)}) collective-permute-start(bf16[1,1024,128]{2,1,0:T(8,128)(2,1)S(1)} %bitcast.60), channel_id=1, source_target_pairs={{0,16},{16,32},{32,48},{48,64},{64,80},{80,96},{96,112},{112,128},... | collective-permute-start | bytes 786440 | tf_op jit(solution)/shard_map/while/body/eval_jaxpr/ppermute | solution.py:14
  130.9 5.6 %collective-permute-start = (bf16[1,1024,128]{2,1,0:T(8,128)(2,1)S(1)}, bf16[1,1024,128]{2,1,0:T(8,128)(2,1)S(1)}, u32[]{:S(2)}, u32[]{:S(2)}) collective-permute-start(bf16[1,1024,128]{2,1,0:T(8,128)(2,1)S(1)} %get-tuple-element.627), channel_id=1, source_target_pairs={{1,0},{2,1},{3,2},{4,3},{5,4},{6,5},{7,6},{8,7},{9,8},{10,9},{11,1... | collective-permute-start | bytes 786440 | tf_op jit(solution)/shard_map/while/body/eval_jaxpr/ppermute | solution.py:17
  141.3 7.1 %collective-permute-start.2 = (bf16[1,1024,128]{2,1,0:T(8,128)(2,1)S(1)}, bf16[1,1024,128]{2,1,0:T(8,128)(2,1)S(1)}, u32[]{:S(2)}, u32[]{:S(2)}) collective-permute-start(bf16[1,1024,128]{2,1,0:T(8,128)(2,1)S(1)} %bitcast.60), channel_id=1, source_target_pairs={{0,16},{16,32},{32,48},{48,64},{64,80},{80,96},{96,112},{112,128},... | collective-permute-start | bytes 786440 | tf_op jit(solution)/shard_map/while/body/eval_jaxpr/ppermute | solution.py:14
  156.2 5.5 collective-permute-start
  161.7 1.9 collective-permute-done
  166.4 7.1 %collective-permute-start.2 = (bf16[1,1024,128]{2,1,0:T(8,128)(2,1)S(1)}, bf16[1,1024,128]{2,1,0:T(8,128)(2,1)S(1)}, u32[]{:S(2)}, u32[]{:S(2)}) collective-permute-start(bf16[1,1024,128]{2,1,0:T(8,128)(2,1)S(1)} %bitcast.60), channel_id=1, source_target_pairs={{0,16},{16,32},{32,48},{48,64},{64,80},{80,96},{96,112},{112,128},... | collective-permute-start | bytes 786440 | tf_op jit(solution)/shard_map/while/body/eval_jaxpr/ppermute | solution.py:14
  181.4 5.5 collective-permute-start
  186.9 1.9 collective-permute-done
  191.6 7.1 %collective-permute-start.2 = (bf16[1,1024,128]{2,1,0:T(8,128)(2,1)S(1)}, bf16[1,1024,128]{2,1,0:T(8,128)(2,1)S(1)}, u32[]{:S(2)}, u32[]{:S(2)}) collective-permute-start(bf16[1,1024,128]{2,1,0:T(8,128)(2,1)S(1)} %bitcast.60), channel_id=1, source_target_pairs={{0,16},{16,32},{32,48},{48,64},{64,80},{80,96},{96,112},{112,128},... | collective-permute-start | bytes 786440 | tf_op jit(solution)/shard_map/while/body/eval_jaxpr/ppermute | solution.py:14
  206.6 5.4 collective-permute-start
  212.0 2.0 collective-permute-done
  216.7 7.2 %collective-permute-start.2 = (bf16[1,1024,128]{2,1,0:T(8,128)(2,1)S(1)}, bf16[1,1024,128]{2,1,0:T(8,128)(2,1)S(1)}, u32[]{:S(2)}, u32[]{:S(2)}) collective-permute-start(bf16[1,1024,128]{2,1,0:T(8,128)(2,1)S(1)} %bitcast.60), channel_id=1, source_target_pairs={{0,16},{16,32},{32,48},{48,64},{64,80},{80,96},{96,112},{112,128},... | collective-permute-start | bytes 786440 | tf_op jit(solution)/shard_map/while/body/eval_jaxpr/ppermute | solution.py:14
  231.7 5.4 collective-permute-start
  237.1 2.0 collective-permute-done
  241.8 7.1 %collective-permute-start.2 = (bf16[1,1024,128]{2,1,0:T(8,128)(2,1)S(1)}, bf16[1,1024,128]{2,1,0:T(8,128)(2,1)S(1)}, u32[]{:S(2)}, u32[]{:S(2)}) collective-permute-start(bf16[1,1024,128]{2,1,0:T(8,128)(2,1)S(1)} %bitcast.60), channel_id=1, source_target_pairs={{0,16},{16,32},{32,48},{48,64},{64,80},{80,96},{96,112},{112,128},... | collective-permute-start | bytes 786440 | tf_op jit(solution)/shard_map/while/body/eval_jaxpr/ppermute | solution.py:14
  256.8 5.3 collective-permute-start
  262.1 2.1 collective-permute-done
  266.9 7.2 %collective-permute-start.2 = (bf16[1,1024,128]{2,1,0:T(8,128)(2,1)S(1)}, bf16[1,1024,128]{2,1,0:T(8,128)(2,1)S(1)}, u32[]{:S(2)}, u32[]{:S(2)}) collective-permute-start(bf16[1,1024,128]{2,1,0:T(8,128)(2,1)S(1)} %bitcast.60), channel_id=1, source_target_pairs={{0,16},{16,32},{32,48},{48,64},{64,80},{80,96},{96,112},{112,128},... | collective-permute-start | bytes 786440 | tf_op jit(solution)/shard_map/while/body/eval_jaxpr/ppermute | solution.py:14
  281.9 5.3 collective-permute-start
  287.1 2.1 collective-permute-done
  291.9 7.2 %collective-permute-start.2 = (bf16[1,1024,128]{2,1,0:T(8,128)(2,1)S(1)}, bf16[1,1024,128]{2,1,0:T(8,128)(2,1)S(1)}, u32[]{:S(2)}, u32[]{:S(2)}) collective-permute-start(bf16[1,1024,128]{2,1,0:T(8,128)(2,1)S(1)} %bitcast.60), channel_id=1, source_target_pairs={{0,16},{16,32},{32,48},{48,64},{64,80},{80,96},{96,112},{112,128},... | collective-permute-start | bytes 786440 | tf_op jit(solution)/shard_map/while/body/eval_jaxpr/ppermute | solution.py:14
  306.9 5.2 collective-permute-start
  312.2 2.2 collective-permute-done
  316.9 7.2 %collective-permute-start.2 = (bf16[1,1024,128]{2,1,0:T(8,128)(2,1)S(1)}, bf16[1,1024,128]{2,1,0:T(8,128)(2,1)S(1)}, u32[]{:S(2)}, u32[]{:S(2)}) collective-permute-start(bf16[1,1024,128]{2,1,0:T(8,128)(2,1)S(1)} %bitcast.60), channel_id=1, source_target_pairs={{0,16},{16,32},{32,48},{48,64},{64,80},{80,96},{96,112},{112,128},... | collective-permute-start | bytes 786440 | tf_op jit(solution)/shard_map/while/body/eval_jaxpr/ppermute | solution.py:14
  331.9 5.2 collective-permute-start
  337.1 2.2 collective-permute-done
  341.8 7.1 %collective-permute-start.2 = (bf16[1,1024,128]{2,1,0:T(8,128)(2,1)S(1)}, bf16[1,1024,128]{2,1,0:T(8,128)(2,1)S(1)}, u32[]{:S(2)}, u32[]{:S(2)}) collective-permute-start(bf16[1,1024,128]{2,1,0:T(8,128)(2,1)S(1)} %bitcast.60), channel_id=1, source_target_pairs={{0,16},{16,32},{32,48},{48,64},{64,80},{80,96},{96,112},{112,128},... | collective-permute-start | bytes 786440 | tf_op jit(solution)/shard_map/while/body/eval_jaxpr/ppermute | solution.py:14
  356.8 5.1 collective-permute-start
  362.0 2.3 collective-permute-done
  366.7 7.2 %collective-permute-start.2 = (bf16[1,1024,128]{2,1,0:T(8,128)(2,1)S(1)}, bf16[1,1024,128]{2,1,0:T(8,128)(2,1)S(1)}, u32[]{:S(2)}, u32[]{:S(2)}) collective-permute-start(bf16[1,1024,128]{2,1,0:T(8,128)(2,1)S(1)} %bitcast.60), channel_id=1, source_target_pairs={{0,16},{16,32},{32,48},{48,64},{64,80},{80,96},{96,112},{112,128},... | collective-permute-start | bytes 786440 | tf_op jit(solution)/shard_map/while/body/eval_jaxpr/ppermute | solution.py:14
  381.7 5.1 collective-permute-start
  386.8 2.3 collective-permute-done
  391.6 7.2 %collective-permute-start.2 = (bf16[1,1024,128]{2,1,0:T(8,128)(2,1)S(1)}, bf16[1,1024,128]{2,1,0:T(8,128)(2,1)S(1)}, u32[]{:S(2)}, u32[]{:S(2)}) collective-permute-start(bf16[1,1024,128]{2,1,0:T(8,128)(2,1)S(1)} %bitcast.60), channel_id=1, source_target_pairs={{0,16},{16,32},{32,48},{48,64},{64,80},{80,96},{96,112},{112,128},... | collective-permute-start | bytes 786440 | tf_op jit(solution)/shard_map/while/body/eval_jaxpr/ppermute | solution.py:14
  403.0 145.6 %all-gather.3.cloned.1.call-done = f32[524288]{0:T(1024)} async-done(((f32[1024]{0:T(1024)}), f32[524288]{0:T(1024)}) %all-gather.3.cloned.1.call-update) | async-done | bytes 2097168 | tf_op jit(solution)/shard_map/all_gather | solution.py:123
  (346 shorter events, 203.1 us)
Async XLA Ops:
  6.5 542.1 %all-gather.3.cloned.1.call-start = ((), (), s32[]{:S(2)}) async-start(), calls=%async_computation | async-start | bytes 2101248 | tf_op jit(solution)/shard_map/all_gather | solution.py:123
  10.7 8.0 %collective-permute-start = (bf16[1,1024,128]{2,1,0:T(8,128)(2,1)S(1)}, bf16[1,1024,128]{2,1,0:T(8,128)(2,1)S(1)}, u32[]{:S(2)}, u32[]{:S(2)}) collective-permute-start(bf16[1,1024,128]{2,1,0:T(8,128)(2,1)S(1)} %get-tuple-element.627), channel_id=1, source_target_pairs={{1,0},{2,1},{3,2},{4,3},{5,4},{6,5},{7,6},{8,7},{9,8},{10,9},{11,1... | collective-permute-start | bytes 786440 | tf_op jit(solution)/shard_map/while/body/eval_jaxpr/ppermute | solution.py:17
  23.1 7.3 %collective-permute-start.2 = (bf16[1,1024,128]{2,1,0:T(8,128)(2,1)S(1)}, bf16[1,1024,128]{2,1,0:T(8,128)(2,1)S(1)}, u32[]{:S(2)}, u32[]{:S(2)}) collective-permute-start(bf16[1,1024,128]{2,1,0:T(8,128)(2,1)S(1)} %bitcast.60), channel_id=1, source_target_pairs={{0,16},{16,32},{32,48},{48,64},{64,80},{80,96},{96,112},{112,128},... | collective-permute-start | bytes 786440 | tf_op jit(solution)/shard_map/while/body/eval_jaxpr/ppermute | solution.py:14
  35.0 8.3 %collective-permute-start = (bf16[1,1024,128]{2,1,0:T(8,128)(2,1)S(1)}, bf16[1,1024,128]{2,1,0:T(8,128)(2,1)S(1)}, u32[]{:S(2)}, u32[]{:S(2)}) collective-permute-start(bf16[1,1024,128]{2,1,0:T(8,128)(2,1)S(1)} %get-tuple-element.627), channel_id=1, source_target_pairs={{1,0},{2,1},{3,2},{4,3},{5,4},{6,5},{7,6},{8,7},{9,8},{10,9},{11,1... | collective-permute-start | bytes 786440 | tf_op jit(solution)/shard_map/while/body/eval_jaxpr/ppermute | solution.py:17
  45.6 7.9 %collective-permute-start.3 = (bf16[1,1024,128]{2,1,0:T(8,128)(2,1)S(1)}, bf16[1,1024,128]{2,1,0:T(8,128)(2,1)S(1)}, u32[]{:S(2)}, u32[]{:S(2)}) collective-permute-start(bf16[1,1024,128]{2,1,0:T(8,128)(2,1)S(1)} %bitcast.59), channel_id=1, source_target_pairs={{16,0},{32,16},{48,32},{64,48},{80,64},{96,80},{112,96},{128,112},... | collective-permute-start | bytes 786440 | tf_op jit(solution)/shard_map/while/body/eval_jaxpr/ppermute | solution.py:17
  46.9 8.0 %collective-permute-start.2 = (bf16[1,1024,128]{2,1,0:T(8,128)(2,1)S(1)}, bf16[1,1024,128]{2,1,0:T(8,128)(2,1)S(1)}, u32[]{:S(2)}, u32[]{:S(2)}) collective-permute-start(bf16[1,1024,128]{2,1,0:T(8,128)(2,1)S(1)} %bitcast.60), channel_id=1, source_target_pairs={{0,16},{16,32},{32,48},{48,64},{64,80},{80,96},{96,112},{112,128},... | collective-permute-start | bytes 786440 | tf_op jit(solution)/shard_map/while/body/eval_jaxpr/ppermute | solution.py:14
  59.4 7.4 %collective-permute-start = (bf16[1,1024,128]{2,1,0:T(8,128)(2,1)S(1)}, bf16[1,1024,128]{2,1,0:T(8,128)(2,1)S(1)}, u32[]{:S(2)}, u32[]{:S(2)}) collective-permute-start(bf16[1,1024,128]{2,1,0:T(8,128)(2,1)S(1)} %get-tuple-element.627), channel_id=1, source_target_pairs={{1,0},{2,1},{3,2},{4,3},{5,4},{6,5},{7,6},{8,7},{9,8},{10,9},{11,1... | collective-permute-start | bytes 786440 | tf_op jit(solution)/shard_map/while/body/eval_jaxpr/ppermute | solution.py:17
  68.9 7.9 %collective-permute-start.3 = (bf16[1,1024,128]{2,1,0:T(8,128)(2,1)S(1)}, bf16[1,1024,128]{2,1,0:T(8,128)(2,1)S(1)}, u32[]{:S(2)}, u32[]{:S(2)}) collective-permute-start(bf16[1,1024,128]{2,1,0:T(8,128)(2,1)S(1)} %bitcast.59), channel_id=1, source_target_pairs={{16,0},{32,16},{48,32},{64,48},{80,64},{96,80},{112,96},{128,112},... | collective-permute-start | bytes 786440 | tf_op jit(solution)/shard_map/while/body/eval_jaxpr/ppermute | solution.py:17
  70.2 8.0 %collective-permute-start.2 = (bf16[1,1024,128]{2,1,0:T(8,128)(2,1)S(1)}, bf16[1,1024,128]{2,1,0:T(8,128)(2,1)S(1)}, u32[]{:S(2)}, u32[]{:S(2)}) collective-permute-start(bf16[1,1024,128]{2,1,0:T(8,128)(2,1)S(1)} %bitcast.60), channel_id=1, source_target_pairs={{0,16},{16,32},{32,48},{48,64},{64,80},{80,96},{96,112},{112,128},... | collective-permute-start | bytes 786440 | tf_op jit(solution)/shard_map/while/body/eval_jaxpr/ppermute | solution.py:14
  82.8 7.5 %collective-permute-start = (bf16[1,1024,128]{2,1,0:T(8,128)(2,1)S(1)}, bf16[1,1024,128]{2,1,0:T(8,128)(2,1)S(1)}, u32[]{:S(2)}, u32[]{:S(2)}) collective-permute-start(bf16[1,1024,128]{2,1,0:T(8,128)(2,1)S(1)} %get-tuple-element.627), channel_id=1, source_target_pairs={{1,0},{2,1},{3,2},{4,3},{5,4},{6,5},{7,6},{8,7},{9,8},{10,9},{11,1... | collective-permute-start | bytes 786440 | tf_op jit(solution)/shard_map/while/body/eval_jaxpr/ppermute | solution.py:17
  92.5 7.9 %collective-permute-start.3 = (bf16[1,1024,128]{2,1,0:T(8,128)(2,1)S(1)}, bf16[1,1024,128]{2,1,0:T(8,128)(2,1)S(1)}, u32[]{:S(2)}, u32[]{:S(2)}) collective-permute-start(bf16[1,1024,128]{2,1,0:T(8,128)(2,1)S(1)} %bitcast.59), channel_id=1, source_target_pairs={{16,0},{32,16},{48,32},{64,48},{80,64},{96,80},{112,96},{128,112},... | collective-permute-start | bytes 786440 | tf_op jit(solution)/shard_map/while/body/eval_jaxpr/ppermute | solution.py:17
  93.8 8.0 %collective-permute-start.2 = (bf16[1,1024,128]{2,1,0:T(8,128)(2,1)S(1)}, bf16[1,1024,128]{2,1,0:T(8,128)(2,1)S(1)}, u32[]{:S(2)}, u32[]{:S(2)}) collective-permute-start(bf16[1,1024,128]{2,1,0:T(8,128)(2,1)S(1)} %bitcast.60), channel_id=1, source_target_pairs={{0,16},{16,32},{32,48},{48,64},{64,80},{80,96},{96,112},{112,128},... | collective-permute-start | bytes 786440 | tf_op jit(solution)/shard_map/while/body/eval_jaxpr/ppermute | solution.py:14
  106.4 7.4 %collective-permute-start = (bf16[1,1024,128]{2,1,0:T(8,128)(2,1)S(1)}, bf16[1,1024,128]{2,1,0:T(8,128)(2,1)S(1)}, u32[]{:S(2)}, u32[]{:S(2)}) collective-permute-start(bf16[1,1024,128]{2,1,0:T(8,128)(2,1)S(1)} %get-tuple-element.627), channel_id=1, source_target_pairs={{1,0},{2,1},{3,2},{4,3},{5,4},{6,5},{7,6},{8,7},{9,8},{10,9},{11,1... | collective-permute-start | bytes 786440 | tf_op jit(solution)/shard_map/while/body/eval_jaxpr/ppermute | solution.py:17
  115.7 9.1 %collective-permute-start.3 = (bf16[1,1024,128]{2,1,0:T(8,128)(2,1)S(1)}, bf16[1,1024,128]{2,1,0:T(8,128)(2,1)S(1)}, u32[]{:S(2)}, u32[]{:S(2)}) collective-permute-start(bf16[1,1024,128]{2,1,0:T(8,128)(2,1)S(1)} %bitcast.59), channel_id=1, source_target_pairs={{16,0},{32,16},{48,32},{64,48},{80,64},{96,80},{112,96},{128,112},... | collective-permute-start | bytes 786440 | tf_op jit(solution)/shard_map/while/body/eval_jaxpr/ppermute | solution.py:17
  117.0 9.3 %collective-permute-start.2 = (bf16[1,1024,128]{2,1,0:T(8,128)(2,1)S(1)}, bf16[1,1024,128]{2,1,0:T(8,128)(2,1)S(1)}, u32[]{:S(2)}, u32[]{:S(2)}) collective-permute-start(bf16[1,1024,128]{2,1,0:T(8,128)(2,1)S(1)} %bitcast.60), channel_id=1, source_target_pairs={{0,16},{16,32},{32,48},{48,64},{64,80},{80,96},{96,112},{112,128},... | collective-permute-start | bytes 786440 | tf_op jit(solution)/shard_map/while/body/eval_jaxpr/ppermute | solution.py:14
  130.9 7.4 %collective-permute-start = (bf16[1,1024,128]{2,1,0:T(8,128)(2,1)S(1)}, bf16[1,1024,128]{2,1,0:T(8,128)(2,1)S(1)}, u32[]{:S(2)}, u32[]{:S(2)}) collective-permute-start(bf16[1,1024,128]{2,1,0:T(8,128)(2,1)S(1)} %get-tuple-element.627), channel_id=1, source_target_pairs={{1,0},{2,1},{3,2},{4,3},{5,4},{6,5},{7,6},{8,7},{9,8},{10,9},{11,1... | collective-permute-start | bytes 786440 | tf_op jit(solution)/shard_map/while/body/eval_jaxpr/ppermute | solution.py:17
  140.0 10.2 %collective-permute-start.3 = (bf16[1,1024,128]{2,1,0:T(8,128)(2,1)S(1)}, bf16[1,1024,128]{2,1,0:T(8,128)(2,1)S(1)}, u32[]{:S(2)}, u32[]{:S(2)}) collective-permute-start(bf16[1,1024,128]{2,1,0:T(8,128)(2,1)S(1)} %bitcast.59), channel_id=1, source_target_pairs={{16,0},{32,16},{48,32},{64,48},{80,64},{96,80},{112,96},{128,112},... | collective-permute-start | bytes 786440 | tf_op jit(solution)/shard_map/while/body/eval_jaxpr/ppermute | solution.py:17
  141.3 10.4 %collective-permute-start.2 = (bf16[1,1024,128]{2,1,0:T(8,128)(2,1)S(1)}, bf16[1,1024,128]{2,1,0:T(8,128)(2,1)S(1)}, u32[]{:S(2)}, u32[]{:S(2)}) collective-permute-start(bf16[1,1024,128]{2,1,0:T(8,128)(2,1)S(1)} %bitcast.60), channel_id=1, source_target_pairs={{0,16},{16,32},{32,48},{48,64},{64,80},{80,96},{96,112},{112,128},... | collective-permute-start | bytes 786440 | tf_op jit(solution)/shard_map/while/body/eval_jaxpr/ppermute | solution.py:14
  156.2 7.4 %collective-permute-start = (bf16[1,1024,128]{2,1,0:T(8,128)(2,1)S(1)}, bf16[1,1024,128]{2,1,0:T(8,128)(2,1)S(1)}, u32[]{:S(2)}, u32[]{:S(2)}) collective-permute-start(bf16[1,1024,128]{2,1,0:T(8,128)(2,1)S(1)} %get-tuple-element.627), channel_id=1, source_target_pairs={{1,0},{2,1},{3,2},{4,3},{5,4},{6,5},{7,6},{8,7},{9,8},{10,9},{11,1... | collective-permute-start | bytes 786440 | tf_op jit(solution)/shard_map/while/body/eval_jaxpr/ppermute | solution.py:17
  165.1 10.3 %collective-permute-start.3 = (bf16[1,1024,128]{2,1,0:T(8,128)(2,1)S(1)}, bf16[1,1024,128]{2,1,0:T(8,128)(2,1)S(1)}, u32[]{:S(2)}, u32[]{:S(2)}) collective-permute-start(bf16[1,1024,128]{2,1,0:T(8,128)(2,1)S(1)} %bitcast.59), channel_id=1, source_target_pairs={{16,0},{32,16},{48,32},{64,48},{80,64},{96,80},{112,96},{128,112},... | collective-permute-start | bytes 786440 | tf_op jit(solution)/shard_map/while/body/eval_jaxpr/ppermute | solution.py:17
  166.4 10.4 %collective-permute-start.2 = (bf16[1,1024,128]{2,1,0:T(8,128)(2,1)S(1)}, bf16[1,1024,128]{2,1,0:T(8,128)(2,1)S(1)}, u32[]{:S(2)}, u32[]{:S(2)}) collective-permute-start(bf16[1,1024,128]{2,1,0:T(8,128)(2,1)S(1)} %bitcast.60), channel_id=1, source_target_pairs={{0,16},{16,32},{32,48},{48,64},{64,80},{80,96},{96,112},{112,128},... | collective-permute-start | bytes 786440 | tf_op jit(solution)/shard_map/while/body/eval_jaxpr/ppermute | solution.py:14
  181.4 7.4 %collective-permute-start = (bf16[1,1024,128]{2,1,0:T(8,128)(2,1)S(1)}, bf16[1,1024,128]{2,1,0:T(8,128)(2,1)S(1)}, u32[]{:S(2)}, u32[]{:S(2)}) collective-permute-start(bf16[1,1024,128]{2,1,0:T(8,128)(2,1)S(1)} %get-tuple-element.627), channel_id=1, source_target_pairs={{1,0},{2,1},{3,2},{4,3},{5,4},{6,5},{7,6},{8,7},{9,8},{10,9},{11,1... | collective-permute-start | bytes 786440 | tf_op jit(solution)/shard_map/while/body/eval_jaxpr/ppermute | solution.py:17
  190.3 10.2 %collective-permute-start.3 = (bf16[1,1024,128]{2,1,0:T(8,128)(2,1)S(1)}, bf16[1,1024,128]{2,1,0:T(8,128)(2,1)S(1)}, u32[]{:S(2)}, u32[]{:S(2)}) collective-permute-start(bf16[1,1024,128]{2,1,0:T(8,128)(2,1)S(1)} %bitcast.59), channel_id=1, source_target_pairs={{16,0},{32,16},{48,32},{64,48},{80,64},{96,80},{112,96},{128,112},... | collective-permute-start | bytes 786440 | tf_op jit(solution)/shard_map/while/body/eval_jaxpr/ppermute | solution.py:17
  191.6 10.4 %collective-permute-start.2 = (bf16[1,1024,128]{2,1,0:T(8,128)(2,1)S(1)}, bf16[1,1024,128]{2,1,0:T(8,128)(2,1)S(1)}, u32[]{:S(2)}, u32[]{:S(2)}) collective-permute-start(bf16[1,1024,128]{2,1,0:T(8,128)(2,1)S(1)} %bitcast.60), channel_id=1, source_target_pairs={{0,16},{16,32},{32,48},{48,64},{64,80},{80,96},{96,112},{112,128},... | collective-permute-start | bytes 786440 | tf_op jit(solution)/shard_map/while/body/eval_jaxpr/ppermute | solution.py:14
  206.6 7.4 %collective-permute-start = (bf16[1,1024,128]{2,1,0:T(8,128)(2,1)S(1)}, bf16[1,1024,128]{2,1,0:T(8,128)(2,1)S(1)}, u32[]{:S(2)}, u32[]{:S(2)}) collective-permute-start(bf16[1,1024,128]{2,1,0:T(8,128)(2,1)S(1)} %get-tuple-element.627), channel_id=1, source_target_pairs={{1,0},{2,1},{3,2},{4,3},{5,4},{6,5},{7,6},{8,7},{9,8},{10,9},{11,1... | collective-permute-start | bytes 786440 | tf_op jit(solution)/shard_map/while/body/eval_jaxpr/ppermute | solution.py:17
  215.4 10.3 %collective-permute-start.3 = (bf16[1,1024,128]{2,1,0:T(8,128)(2,1)S(1)}, bf16[1,1024,128]{2,1,0:T(8,128)(2,1)S(1)}, u32[]{:S(2)}, u32[]{:S(2)}) collective-permute-start(bf16[1,1024,128]{2,1,0:T(8,128)(2,1)S(1)} %bitcast.59), channel_id=1, source_target_pairs={{16,0},{32,16},{48,32},{64,48},{80,64},{96,80},{112,96},{128,112},... | collective-permute-start | bytes 786440 | tf_op jit(solution)/shard_map/while/body/eval_jaxpr/ppermute | solution.py:17
  216.7 10.5 %collective-permute-start.2 = (bf16[1,1024,128]{2,1,0:T(8,128)(2,1)S(1)}, bf16[1,1024,128]{2,1,0:T(8,128)(2,1)S(1)}, u32[]{:S(2)}, u32[]{:S(2)}) collective-permute-start(bf16[1,1024,128]{2,1,0:T(8,128)(2,1)S(1)} %bitcast.60), channel_id=1, source_target_pairs={{0,16},{16,32},{32,48},{48,64},{64,80},{80,96},{96,112},{112,128},... | collective-permute-start | bytes 786440 | tf_op jit(solution)/shard_map/while/body/eval_jaxpr/ppermute | solution.py:14
  231.7 7.4 %collective-permute-start = (bf16[1,1024,128]{2,1,0:T(8,128)(2,1)S(1)}, bf16[1,1024,128]{2,1,0:T(8,128)(2,1)S(1)}, u32[]{:S(2)}, u32[]{:S(2)}) collective-permute-start(bf16[1,1024,128]{2,1,0:T(8,128)(2,1)S(1)} %get-tuple-element.627), channel_id=1, source_target_pairs={{1,0},{2,1},{3,2},{4,3},{5,4},{6,5},{7,6},{8,7},{9,8},{10,9},{11,1... | collective-permute-start | bytes 786440 | tf_op jit(solution)/shard_map/while/body/eval_jaxpr/ppermute | solution.py:17
  240.5 10.2 %collective-permute-start.3 = (bf16[1,1024,128]{2,1,0:T(8,128)(2,1)S(1)}, bf16[1,1024,128]{2,1,0:T(8,128)(2,1)S(1)}, u32[]{:S(2)}, u32[]{:S(2)}) collective-permute-start(bf16[1,1024,128]{2,1,0:T(8,128)(2,1)S(1)} %bitcast.59), channel_id=1, source_target_pairs={{16,0},{32,16},{48,32},{64,48},{80,64},{96,80},{112,96},{128,112},... | collective-permute-start | bytes 786440 | tf_op jit(solution)/shard_map/while/body/eval_jaxpr/ppermute | solution.py:17
  241.8 10.4 %collective-permute-start.2 = (bf16[1,1024,128]{2,1,0:T(8,128)(2,1)S(1)}, bf16[1,1024,128]{2,1,0:T(8,128)(2,1)S(1)}, u32[]{:S(2)}, u32[]{:S(2)}) collective-permute-start(bf16[1,1024,128]{2,1,0:T(8,128)(2,1)S(1)} %bitcast.60), channel_id=1, source_target_pairs={{0,16},{16,32},{32,48},{48,64},{64,80},{80,96},{96,112},{112,128},... | collective-permute-start | bytes 786440 | tf_op jit(solution)/shard_map/while/body/eval_jaxpr/ppermute | solution.py:14
  256.8 7.4 %collective-permute-start = (bf16[1,1024,128]{2,1,0:T(8,128)(2,1)S(1)}, bf16[1,1024,128]{2,1,0:T(8,128)(2,1)S(1)}, u32[]{:S(2)}, u32[]{:S(2)}) collective-permute-start(bf16[1,1024,128]{2,1,0:T(8,128)(2,1)S(1)} %get-tuple-element.627), channel_id=1, source_target_pairs={{1,0},{2,1},{3,2},{4,3},{5,4},{6,5},{7,6},{8,7},{9,8},{10,9},{11,1... | collective-permute-start | bytes 786440 | tf_op jit(solution)/shard_map/while/body/eval_jaxpr/ppermute | solution.py:17
  265.6 10.3 %collective-permute-start.3 = (bf16[1,1024,128]{2,1,0:T(8,128)(2,1)S(1)}, bf16[1,1024,128]{2,1,0:T(8,128)(2,1)S(1)}, u32[]{:S(2)}, u32[]{:S(2)}) collective-permute-start(bf16[1,1024,128]{2,1,0:T(8,128)(2,1)S(1)} %bitcast.59), channel_id=1, source_target_pairs={{16,0},{32,16},{48,32},{64,48},{80,64},{96,80},{112,96},{128,112},... | collective-permute-start | bytes 786440 | tf_op jit(solution)/shard_map/while/body/eval_jaxpr/ppermute | solution.py:17
  266.9 10.5 %collective-permute-start.2 = (bf16[1,1024,128]{2,1,0:T(8,128)(2,1)S(1)}, bf16[1,1024,128]{2,1,0:T(8,128)(2,1)S(1)}, u32[]{:S(2)}, u32[]{:S(2)}) collective-permute-start(bf16[1,1024,128]{2,1,0:T(8,128)(2,1)S(1)} %bitcast.60), channel_id=1, source_target_pairs={{0,16},{16,32},{32,48},{48,64},{64,80},{80,96},{96,112},{112,128},... | collective-permute-start | bytes 786440 | tf_op jit(solution)/shard_map/while/body/eval_jaxpr/ppermute | solution.py:14
  281.9 7.4 %collective-permute-start = (bf16[1,1024,128]{2,1,0:T(8,128)(2,1)S(1)}, bf16[1,1024,128]{2,1,0:T(8,128)(2,1)S(1)}, u32[]{:S(2)}, u32[]{:S(2)}) collective-permute-start(bf16[1,1024,128]{2,1,0:T(8,128)(2,1)S(1)} %get-tuple-element.627), channel_id=1, source_target_pairs={{1,0},{2,1},{3,2},{4,3},{5,4},{6,5},{7,6},{8,7},{9,8},{10,9},{11,1... | collective-permute-start | bytes 786440 | tf_op jit(solution)/shard_map/while/body/eval_jaxpr/ppermute | solution.py:17
  290.6 10.3 %collective-permute-start.3 = (bf16[1,1024,128]{2,1,0:T(8,128)(2,1)S(1)}, bf16[1,1024,128]{2,1,0:T(8,128)(2,1)S(1)}, u32[]{:S(2)}, u32[]{:S(2)}) collective-permute-start(bf16[1,1024,128]{2,1,0:T(8,128)(2,1)S(1)} %bitcast.59), channel_id=1, source_target_pairs={{16,0},{32,16},{48,32},{64,48},{80,64},{96,80},{112,96},{128,112},... | collective-permute-start | bytes 786440 | tf_op jit(solution)/shard_map/while/body/eval_jaxpr/ppermute | solution.py:17
  291.9 10.5 %collective-permute-start.2 = (bf16[1,1024,128]{2,1,0:T(8,128)(2,1)S(1)}, bf16[1,1024,128]{2,1,0:T(8,128)(2,1)S(1)}, u32[]{:S(2)}, u32[]{:S(2)}) collective-permute-start(bf16[1,1024,128]{2,1,0:T(8,128)(2,1)S(1)} %bitcast.60), channel_id=1, source_target_pairs={{0,16},{16,32},{32,48},{48,64},{64,80},{80,96},{96,112},{112,128},... | collective-permute-start | bytes 786440 | tf_op jit(solution)/shard_map/while/body/eval_jaxpr/ppermute | solution.py:14
  306.9 7.4 %collective-permute-start = (bf16[1,1024,128]{2,1,0:T(8,128)(2,1)S(1)}, bf16[1,1024,128]{2,1,0:T(8,128)(2,1)S(1)}, u32[]{:S(2)}, u32[]{:S(2)}) collective-permute-start(bf16[1,1024,128]{2,1,0:T(8,128)(2,1)S(1)} %get-tuple-element.627), channel_id=1, source_target_pairs={{1,0},{2,1},{3,2},{4,3},{5,4},{6,5},{7,6},{8,7},{9,8},{10,9},{11,1... | collective-permute-start | bytes 786440 | tf_op jit(solution)/shard_map/while/body/eval_jaxpr/ppermute | solution.py:17
  315.6 10.3 %collective-permute-start.3 = (bf16[1,1024,128]{2,1,0:T(8,128)(2,1)S(1)}, bf16[1,1024,128]{2,1,0:T(8,128)(2,1)S(1)}, u32[]{:S(2)}, u32[]{:S(2)}) collective-permute-start(bf16[1,1024,128]{2,1,0:T(8,128)(2,1)S(1)} %bitcast.59), channel_id=1, source_target_pairs={{16,0},{32,16},{48,32},{64,48},{80,64},{96,80},{112,96},{128,112},... | collective-permute-start | bytes 786440 | tf_op jit(solution)/shard_map/while/body/eval_jaxpr/ppermute | solution.py:17
  316.9 10.5 %collective-permute-start.2 = (bf16[1,1024,128]{2,1,0:T(8,128)(2,1)S(1)}, bf16[1,1024,128]{2,1,0:T(8,128)(2,1)S(1)}, u32[]{:S(2)}, u32[]{:S(2)}) collective-permute-start(bf16[1,1024,128]{2,1,0:T(8,128)(2,1)S(1)} %bitcast.60), channel_id=1, source_target_pairs={{0,16},{16,32},{32,48},{48,64},{64,80},{80,96},{96,112},{112,128},... | collective-permute-start | bytes 786440 | tf_op jit(solution)/shard_map/while/body/eval_jaxpr/ppermute | solution.py:14
  331.9 7.4 %collective-permute-start = (bf16[1,1024,128]{2,1,0:T(8,128)(2,1)S(1)}, bf16[1,1024,128]{2,1,0:T(8,128)(2,1)S(1)}, u32[]{:S(2)}, u32[]{:S(2)}) collective-permute-start(bf16[1,1024,128]{2,1,0:T(8,128)(2,1)S(1)} %get-tuple-element.627), channel_id=1, source_target_pairs={{1,0},{2,1},{3,2},{4,3},{5,4},{6,5},{7,6},{8,7},{9,8},{10,9},{11,1... | collective-permute-start | bytes 786440 | tf_op jit(solution)/shard_map/while/body/eval_jaxpr/ppermute | solution.py:17
  340.5 10.3 %collective-permute-start.3 = (bf16[1,1024,128]{2,1,0:T(8,128)(2,1)S(1)}, bf16[1,1024,128]{2,1,0:T(8,128)(2,1)S(1)}, u32[]{:S(2)}, u32[]{:S(2)}) collective-permute-start(bf16[1,1024,128]{2,1,0:T(8,128)(2,1)S(1)} %bitcast.59), channel_id=1, source_target_pairs={{16,0},{32,16},{48,32},{64,48},{80,64},{96,80},{112,96},{128,112},... | collective-permute-start | bytes 786440 | tf_op jit(solution)/shard_map/while/body/eval_jaxpr/ppermute | solution.py:17
  341.8 10.4 %collective-permute-start.2 = (bf16[1,1024,128]{2,1,0:T(8,128)(2,1)S(1)}, bf16[1,1024,128]{2,1,0:T(8,128)(2,1)S(1)}, u32[]{:S(2)}, u32[]{:S(2)}) collective-permute-start(bf16[1,1024,128]{2,1,0:T(8,128)(2,1)S(1)} %bitcast.60), channel_id=1, source_target_pairs={{0,16},{16,32},{32,48},{48,64},{64,80},{80,96},{96,112},{112,128},... | collective-permute-start | bytes 786440 | tf_op jit(solution)/shard_map/while/body/eval_jaxpr/ppermute | solution.py:14
  356.8 7.4 %collective-permute-start = (bf16[1,1024,128]{2,1,0:T(8,128)(2,1)S(1)}, bf16[1,1024,128]{2,1,0:T(8,128)(2,1)S(1)}, u32[]{:S(2)}, u32[]{:S(2)}) collective-permute-start(bf16[1,1024,128]{2,1,0:T(8,128)(2,1)S(1)} %get-tuple-element.627), channel_id=1, source_target_pairs={{1,0},{2,1},{3,2},{4,3},{5,4},{6,5},{7,6},{8,7},{9,8},{10,9},{11,1... | collective-permute-start | bytes 786440 | tf_op jit(solution)/shard_map/while/body/eval_jaxpr/ppermute | solution.py:17
  365.4 10.3 %collective-permute-start.3 = (bf16[1,1024,128]{2,1,0:T(8,128)(2,1)S(1)}, bf16[1,1024,128]{2,1,0:T(8,128)(2,1)S(1)}, u32[]{:S(2)}, u32[]{:S(2)}) collective-permute-start(bf16[1,1024,128]{2,1,0:T(8,128)(2,1)S(1)} %bitcast.59), channel_id=1, source_target_pairs={{16,0},{32,16},{48,32},{64,48},{80,64},{96,80},{112,96},{128,112},... | collective-permute-start | bytes 786440 | tf_op jit(solution)/shard_map/while/body/eval_jaxpr/ppermute | solution.py:17
  366.7 10.5 %collective-permute-start.2 = (bf16[1,1024,128]{2,1,0:T(8,128)(2,1)S(1)}, bf16[1,1024,128]{2,1,0:T(8,128)(2,1)S(1)}, u32[]{:S(2)}, u32[]{:S(2)}) collective-permute-start(bf16[1,1024,128]{2,1,0:T(8,128)(2,1)S(1)} %bitcast.60), channel_id=1, source_target_pairs={{0,16},{16,32},{32,48},{48,64},{64,80},{80,96},{96,112},{112,128},... | collective-permute-start | bytes 786440 | tf_op jit(solution)/shard_map/while/body/eval_jaxpr/ppermute | solution.py:14
  381.7 7.4 %collective-permute-start = (bf16[1,1024,128]{2,1,0:T(8,128)(2,1)S(1)}, bf16[1,1024,128]{2,1,0:T(8,128)(2,1)S(1)}, u32[]{:S(2)}, u32[]{:S(2)}) collective-permute-start(bf16[1,1024,128]{2,1,0:T(8,128)(2,1)S(1)} %get-tuple-element.627), channel_id=1, source_target_pairs={{1,0},{2,1},{3,2},{4,3},{5,4},{6,5},{7,6},{8,7},{9,8},{10,9},{11,1... | collective-permute-start | bytes 786440 | tf_op jit(solution)/shard_map/while/body/eval_jaxpr/ppermute | solution.py:17
  390.3 10.3 %collective-permute-start.3 = (bf16[1,1024,128]{2,1,0:T(8,128)(2,1)S(1)}, bf16[1,1024,128]{2,1,0:T(8,128)(2,1)S(1)}, u32[]{:S(2)}, u32[]{:S(2)}) collective-permute-start(bf16[1,1024,128]{2,1,0:T(8,128)(2,1)S(1)} %bitcast.59), channel_id=1, source_target_pairs={{16,0},{32,16},{48,32},{64,48},{80,64},{96,80},{112,96},{128,112},... | collective-permute-start | bytes 786440 | tf_op jit(solution)/shard_map/while/body/eval_jaxpr/ppermute | solution.py:17
  391.6 10.4 %collective-permute-start.2 = (bf16[1,1024,128]{2,1,0:T(8,128)(2,1)S(1)}, bf16[1,1024,128]{2,1,0:T(8,128)(2,1)S(1)}, u32[]{:S(2)}, u32[]{:S(2)}) collective-permute-start(bf16[1,1024,128]{2,1,0:T(8,128)(2,1)S(1)} %bitcast.60), channel_id=1, source_target_pairs={{0,16},{16,32},{32,48},{48,64},{64,80},{80,96},{96,112},{112,128},... | collective-permute-start | bytes 786440 | tf_op jit(solution)/shard_map/while/body/eval_jaxpr/ppermute | solution.py:14
  (18 other events, 61.7 us)
Sparse Core Ops, SparseCore 0:
  403.2 145.4 all-gather.2
